TPU v7x, 32 devices: a whole 2x2x4 slice. The times are simulated.
32 devices in a mesh: tm: 8 (over z, y), lm: 4 (over x, core).
Axes of the slice: x: 2, y: 2, z: 4, core: 2. Of those that a mesh axis runs over, the one named last changes fastest.
Arguments:
- cam_diag: float32 [12288, 384], P('tm'), as said below
- cam_lower: float32 [12288, 384], P('tm')
- cam_rhs: float32 [32, 384], P('tm'), may hold values from -6 to 6
- obs_cam_jac: float32 [4, 24, 32, 128], P(None, None, 'tm', 'lm'), may hold values from -2 to 2
- obs_point_jac: float32 [4, 3, 32, 128], P(None, None, 'tm', 'lm'), may hold values from -6 to 6
- obs_residual: float32 [4, 32, 128], P(None, 'tm', 'lm'), may hold values from -6 to 6
- point_prior: float32 [32, 128], P('tm', 'lm'), may hold values from 0.2 to 5
- knot_start: int32 [32, 128], P('tm', 'lm'), may hold values from 0 to 63, as said below
Outputs:
- reduced_diag: float32 [3072, 384], P('tm')
- reduced_lower: float32 [3072, 384], P('tm')
- reduced_rhs: float32 [8, 384], P('tm')
Inputs may be any that keep to these rules, and one draw needn't show every extreme that they name: Each 384 x 384 block of cam_diag is symmetric, and the periodic block tridiagonal matrix with diagonal blocks from cam_diag and blocks of cam_lower beside them (block 0 in the corners) is positive definite. A landmark's window covers knots knot_start to knot_start + 3 counted from its segment's first knot; knots past 64 - 1 are the next segment's first ones, those of segment 0 for the last segment.
All inputs are finite; a program needn't handle non-finite values.
Results may differ from a plain program's by a relative error of at most 0.0003.
Values sent between devices are 32-bit elements; how exact they have to be, the bound alone decides.
No kernel may reach another device: no remote copies, remote signals or barrier semaphores. Data moves between devices by JAX's collectives and lax.ppermute only.
A program may use at most 128 MiB of HBM per device.

v0:
```python
import jax
import jax.numpy as jnp
from jax import lax
from jax.sharding import PartitionSpec as P

KNOTS = 64
DOF = 6
ORDER = 4


PRECISE = lax.Precision.HIGHEST


def passed_along(block, axis, distance):
    devices = range(lax.axis_size(axis))
    route = [((i - distance) % len(devices), i) for i in devices]
    return lax.ppermute(block, axis, route)


def point_inverse(normal):
    adj_rows = []
    for row_at in range(3):
        entries = []
        for col_at in range(3):
            entries.append(
                normal[(col_at + 1) % 3, (row_at + 1) % 3]
                * normal[(col_at + 2) % 3, (row_at + 2) % 3]
                - normal[(col_at + 1) % 3, (row_at + 2) % 3]
                * normal[(col_at + 2) % 3, (row_at + 1) % 3]
            )
        adj_rows.append(jnp.stack(entries))
    adjugate = jnp.stack(adj_rows)
    determ = (
        normal[0, 0] * adjugate[0, 0]
        + normal[0, 1] * adjugate[1, 0]
        + normal[0, 2] * adjugate[2, 0]
    )
    return adjugate / determ


def landmark_project(cam_jac, point_jac, residual, prior):
    normal = jnp.einsum("rasl,rbsl->absl", point_jac, point_jac, precision=PRECISE)
    normal = normal + prior[None, None] * jnp.eye(3, dtype=jnp.float32)[:, :, None, None]
    inverse = point_inverse(normal)
    cross = jnp.einsum("rasl,rmsl->amsl", point_jac, cam_jac, precision=PRECISE)
    cross_res = jnp.einsum("rasl,rsl->asl", point_jac, residual, precision=PRECISE)
    solved = jnp.einsum("absl,bmsl->amsl", inverse, cross, precision=PRECISE)
    solved_res = jnp.einsum("absl,bsl->asl", inverse, cross_res, precision=PRECISE)
    projected = cam_jac - jnp.einsum("rasl,amsl->rmsl", point_jac, solved, precision=PRECISE)
    projected_res = residual - jnp.einsum("rasl,asl->rsl", point_jac, solved_res, precision=PRECISE)
    return (projected, projected_res)


def place_knots(values, window_start):
    rows_count = values.shape[0]
    seg_count = values.shape[2]
    group_size = values.shape[3]
    knot_span = KNOTS + ORDER - 1
    offsets = jnp.arange(knot_span, dtype=jnp.int32)[:, None, None] - window_start[None]
    onehot = (offsets[:, None] == jnp.arange(ORDER, dtype=jnp.int32)[None, :, None, None]).astype(
        jnp.float32
    )
    shaped = values.reshape(rows_count, ORDER, DOF, seg_count, group_size)
    placed = jnp.einsum("kosl,rodsl->kdrsl", onehot, shaped, precision=PRECISE)
    return placed.reshape(knot_span * DOF, rows_count, seg_count, group_size)


def batched_terms(cam_jac, point_jac, residual, prior, window_start):
    seg_count = window_start.shape[0]
    landmarks = window_start.shape[1]
    group_size = min(128, landmarks)
    extended = (KNOTS + ORDER - 1) * DOF

    def one_group(totals, group_index):
        projected, projected_res = landmark_project(cam_jac, point_jac, residual, prior)
        placed_cam = place_knots(cam_jac, window_start)
        placed_proj = place_knots(projected, window_start)
        new_mat = totals[0] + jnp.einsum(
            "ersl,frsl->sef", placed_cam, placed_proj, precision=PRECISE
        )
        new_vec = totals[1] + jnp.einsum(
            "ersl,rsl->se", placed_cam, projected_res, precision=PRECISE
        )
        return ((new_mat, new_vec), None)

    start_totals = (
        jnp.zeros((seg_count, extended, extended), jnp.float32),
        jnp.zeros((seg_count, extended), jnp.float32),
    )
    totals, _ = lax.scan(
        one_group, start_totals, jnp.arange(landmarks // group_size, dtype=jnp.int32)
    )
    return totals


def lower_solve(factor, right_hand):
    return jax.scipy.linalg.solve_triangular(factor, right_hand, lower=True)


def eliminate(operands):
    diagonal, coupling, right_side, next_coupling = operands
    factor = jnp.linalg.cholesky(diagonal)
    left_part = lower_solve(factor, coupling)
    right_part = lower_solve(factor, next_coupling.T)
    solved_rhs = lower_solve(factor, right_side[:, None])[:, 0]
    to_next = (
        jnp.dot(right_part.T, right_part, precision=PRECISE),
        jnp.dot(right_part.T, left_part, precision=PRECISE),
        jnp.dot(right_part.T, solved_rhs, precision=PRECISE),
    )
    to_prev = (
        jnp.dot(left_part.T, left_part, precision=PRECISE),
        jnp.dot(left_part.T, solved_rhs, precision=PRECISE),
    )
    return (to_next, to_prev)


def local(
    cam_diag, cam_lower, cam_rhs, obs_cam_jac, obs_point_jac, obs_residual, point_prior, knot_start
):
    blocks = cam_diag.shape[1]
    border = (ORDER - 1) * DOF
    local_count = cam_rhs.shape[0]
    schur_mat, schur_vec = batched_terms(
        obs_cam_jac, obs_point_jac, obs_residual, point_prior, knot_start
    )
    schur_mat, schur_vec = lax.psum((schur_mat, schur_vec), "lm")
    arrived_mat, arrived_vec = passed_along(
        (schur_mat[local_count - 1, blocks:, :], schur_vec[local_count - 1, blocks:]), "tm", 1
    )
    spill_mat = jnp.concatenate([arrived_mat[None], schur_mat[:-1, blocks:, :]], 0)
    spill_vec = jnp.concatenate([arrived_vec[None], schur_vec[:-1, blocks:]], 0)
    diagonal = (
        cam_diag.reshape(local_count, blocks, blocks)
        + schur_mat[:, :blocks, :blocks]
        + jnp.pad(spill_mat[:, :, blocks:], ((0, 0), (0, blocks - border), (0, blocks - border)))
    )
    coupling = cam_lower.reshape(local_count, blocks, blocks) + jnp.pad(
        spill_mat[:, :, :blocks], ((0, 0), (0, blocks - border), (0, 0))
    )
    right_side = (
        cam_rhs - schur_vec[:, :blocks] - jnp.pad(spill_vec, ((0, 0), (0, blocks - border)))
    )
    after_coupling = passed_along(coupling[0], "tm", -1)
    next_first, prev_first = eliminate((diagonal[1], coupling[1], right_side[1], coupling[2]))
    next_last, prev_last = eliminate((diagonal[3], coupling[3], right_side[3], after_coupling))
    mid_diag = diagonal[2] - next_first[0] - prev_last[0]
    mid_coupling = -next_first[1]
    mid_rhs = right_side[2] - next_first[2] - prev_last[1]
    next_mid, prev_mid = eliminate((mid_diag, mid_coupling, mid_rhs, -next_last[1]))
    head_diag = diagonal[0] - prev_first[0] - prev_mid[0]
    head_rhs = right_side[0] - prev_first[1] - prev_mid[1]
    arrived = passed_along(
        (next_last[0] + next_mid[0], next_mid[1], next_last[2] + next_mid[2]), "tm", 1
    )
    out_diag = head_diag - arrived[0]
    out_coupling = -arrived[1]
    out_rhs = head_rhs - arrived[2]
    return (out_diag, out_coupling, out_rhs[None, :])


def solution(mesh):
    placed = (
        P("tm", None),
        P("tm", None),
        P("tm", None),
        P(None, None, "tm", "lm"),
        P(None, None, "tm", "lm"),
        P(None, "tm", "lm"),
        P("tm", "lm"),
        P("tm", "lm"),
    )
    return jax.shard_map(
        local,
        mesh=mesh,
        in_specs=placed,
        out_specs=(P("tm", None), P("tm", None), P("tm", None)),
        check_vma=False,
    )
```

profile of v0, /device:TPU:0, one launch (start us, length us, event | category | flops | bytes accessed | tf_op | source)
XLA Modules:
  0.0 558.1 jit_solution(1726906364949205996)
XLA Ops:
  10.9 4.3 subtract_reduce_fusion.7
  22.5 3.8 copy.135
  39.3 3.6 copy.149
  42.9 8.1 %fusion.4 = f32[4,402,402]{1,2,0:T(8,128)} fusion(f32[402,4,4,32]{0,3,1,2:T(8,128)} %copy.150, f32[402,4,4,32]{3,2,1,0:T(4,128)S(1)} %bitcast.403), kind=kOutput, calls=%fused_computation.15 | convolution fusion | flops 992894976 | bytes 4232256 | tf_op jit(solution)/shard_map/while/body/eval_jaxpr/ersl,frsl->sef/dot_general | solution.py:78
  55.5 8.8 %psum.15 = f32[4,402]{1,0:T(4,128)S(1)} all-reduce(f32[4,402]{1,0:T(4,128)S(1)} %bitcast.414), channel_id=1, replica_groups=mesh['tm'=8,'lm'=4] {'lm'}, use_global_device_ids=true, to_apply=%region_7.10 | all-reduce | flops 1608 | bytes 12864 | tf_op jit(solution)/shard_map/psum | solution.py:127
  65.9 3.2 copy.153
  71.8 54.0 %all-reduce.6.cloned.1.call-done = f32[4,402,402]{1,2,0:T(8,128)} async-done(((f32[4,402,402]{1,2,0:T(8,128)}), f32[4,402,402]{1,2,0:T(8,128)}) %all-reduce.6.cloned.1.call-update) | async-done | bytes 2585680 | tf_op jit(solution)/shard_map/psum | solution.py:127
  130.3 6.3 %collective-permute-done = f32[18,402]{0,1:T(8,128)S(1)} collective-permute-done((f32[18,402]{0,1:T(8,128)S(1)}, f32[18,402]{0,1:T(8,128)S(1)}, u32[]{:S(2)}, u32[]{:S(2)}) %collective-permute-start) | collective-permute-done | bytes 28976 | tf_op jit(solution)/shard_map/ppermute | solution.py:17
  136.7 5.0 fusion.3
  145.8 11.7 %cholesky.273 = f32[128,128]{1,0:T(8,128)S(1)} custom-call(f32[128,128]{1,0:T(8,128)S(1)} %cholesky.428), custom_call_target="Cholesky" | custom-call | tf_op jit(solution)/shard_map/jit(cholesky)/cholesky | solution.py:102
  157.6 9.8 %custom-call.31 = f32[1,128,128]{1,2,0:T(8,128)S(1)} custom-call(f32[1,128,128]{2,1,0:T(8,128)S(1)} %get-tuple-element.179), custom_call_target="InvertDiagBlocksLowerTriangular" | custom-call | tf_op jit(solution)/shard_map/jit(cholesky)/cholesky | solution.py:102
  169.8 11.7 %cholesky.292 = f32[128,128]{1,0:T(8,128)S(1)} custom-call(f32[128,128]{1,0:T(8,128)S(1)} %cholesky.432), custom_call_target="Cholesky" | custom-call | tf_op jit(solution)/shard_map/jit(cholesky)/cholesky | solution.py:102
  182.9 10.0 %custom-call.32 = f32[1,128,128]{1,2,0:T(8,128)S(1)} custom-call(f32[1,128,128]{2,1,0:T(8,128)S(1)} %get-tuple-element.176), custom_call_target="InvertDiagBlocksLowerTriangular" | custom-call | tf_op jit(solution)/shard_map/jit(cholesky)/cholesky | solution.py:102
  194.2 11.7 %cholesky.311 = f32[128,128]{1,0:T(8,128)S(1)} custom-call(f32[128,128]{1,0:T(8,128)S(1)} %convolution_subtract_fusion.9), custom_call_target="Cholesky" | custom-call | tf_op jit(solution)/shard_map/jit(cholesky)/cholesky | solution.py:102
  209.3 6.4 %while.23 = (s32[]{:T(128)}, f32[384,384]{1,0:T(8,128)S(1)}, s32[3,2]{0,1:T(2,128)S(1)}, f32[3,128,128]{2,1,0:T(8,128)S(1)}, s32[]{:T(128)}) while((s32[]{:T(128)}, f32[384,384]{1,0:T(8,128)S(1)}, s32[3,2]{0,1:T(2,128)S(1)}, f32[3,128,128]{2,1,0:T(8,128)S(1)}, s32[]{:T(128)}) %tuple.120), condition=%wide.while_cond, body=%wide.while_body.sunk | while | flops 2 | bytes 131181 | solution.py:97
  215.6 29.7 %custom-call.33 = f32[3,128,128]{1,2,0:T(8,128)S(1)} custom-call(f32[3,128,128]{2,1,0:T(8,128)S(1)} %get-tuple-element.88), custom_call_target="InvertDiagBlocksLowerTriangular" | custom-call | tf_op jit(solution)/shard_map/jit(_solve_triangular)/triangular_solve | solution.py:97
  260.2 11.7 %cholesky.326 = f32[128,128]{1,0:T(8,128)S(1)} custom-call(f32[128,128]{1,0:T(8,128)S(1)} %cholesky.436), custom_call_target="Cholesky" | custom-call | tf_op jit(solution)/shard_map/jit(cholesky)/cholesky | solution.py:102
  272.0 10.3 %custom-call.35 = f32[1,128,128]{1,2,0:T(8,128)S(1)} custom-call(f32[1,128,128]{2,1,0:T(8,128)S(1)} %get-tuple-element.186), custom_call_target="InvertDiagBlocksLowerTriangular" | custom-call | tf_op jit(solution)/shard_map/jit(cholesky)/cholesky | solution.py:102
  284.6 11.7 %cholesky.345 = f32[128,128]{1,0:T(8,128)S(1)} custom-call(f32[128,128]{1,0:T(8,128)S(1)} %cholesky.440), custom_call_target="Cholesky" | custom-call | tf_op jit(solution)/shard_map/jit(cholesky)/cholesky | solution.py:102
  297.6 9.8 %custom-call.36 = f32[1,128,128]{1,2,0:T(8,128)S(1)} custom-call(f32[1,128,128]{2,1,0:T(8,128)S(1)} %get-tuple-element.183), custom_call_target="InvertDiagBlocksLowerTriangular" | custom-call | tf_op jit(solution)/shard_map/jit(cholesky)/cholesky | solution.py:102
  308.8 11.7 %cholesky.364 = f32[128,128]{1,0:T(8,128)S(1)} custom-call(f32[128,128]{1,0:T(8,128)S(1)} %convolution_subtract_fusion.8), custom_call_target="Cholesky" | custom-call | tf_op jit(solution)/shard_map/jit(cholesky)/cholesky | solution.py:102
  323.1 5.7 %while.24 = (s32[]{:T(128)}, f32[384,384]{1,0:T(8,128)S(1)}, s32[3,2]{0,1:T(2,128)S(1)}, f32[3,128,128]{2,1,0:T(8,128)S(1)}, s32[]{:T(128)}) while((s32[]{:T(128)}, f32[384,384]{1,0:T(8,128)S(1)}, s32[3,2]{0,1:T(2,128)S(1)}, f32[3,128,128]{2,1,0:T(8,128)S(1)}, s32[]{:T(128)}) %tuple.128), condition=%wide.while_cond.clone.1, body=%wide.while_body.clone.1.sunk | while | flops 2 | bytes 131181 | solution.py:97
  328.8 29.7 %custom-call.37 = f32[3,128,128]{1,2,0:T(8,128)S(1)} custom-call(f32[3,128,128]{2,1,0:T(8,128)S(1)} %get-tuple-element.90), custom_call_target="InvertDiagBlocksLowerTriangular" | custom-call | tf_op jit(solution)/shard_map/jit(_solve_triangular)/triangular_solve | solution.py:97
  370.9 11.7 %cholesky.379 = f32[128,128]{1,0:T(8,128)S(1)} custom-call(f32[128,128]{1,0:T(8,128)S(1)} %cholesky.444), custom_call_target="Cholesky" | custom-call | tf_op jit(solution)/shard_map/jit(cholesky)/cholesky | solution.py:102
  385.2 11.3 %custom-call.38 = f32[1,128,128]{1,2,0:T(8,128)} custom-call(f32[1,128,128]{2,1,0:T(8,128)} %get-tuple-element.172), custom_call_target="InvertDiagBlocksLowerTriangular" | custom-call | tf_op jit(solution)/shard_map/jit(cholesky)/cholesky | solution.py:102
  400.1 13.4 %cholesky.398 = f32[128,128]{1,0:T(8,128)} custom-call(f32[128,128]{1,0:T(8,128)} %cholesky.448), custom_call_target="Cholesky" | custom-call | tf_op jit(solution)/shard_map/jit(cholesky)/cholesky | solution.py:102
  417.0 11.3 %custom-call.39 = f32[1,128,128]{1,2,0:T(8,128)} custom-call(f32[1,128,128]{2,1,0:T(8,128)} %get-tuple-element.169), custom_call_target="InvertDiagBlocksLowerTriangular" | custom-call | tf_op jit(solution)/shard_map/jit(cholesky)/cholesky | solution.py:102
  431.1 13.2 %cholesky.417 = f32[128,128]{1,0:T(8,128)} custom-call(f32[128,128]{1,0:T(8,128)} %convolution_subtract_fusion.7), custom_call_target="Cholesky" | custom-call | tf_op jit(solution)/shard_map/jit(cholesky)/cholesky | solution.py:102
  449.5 7.8 %while.25 = (s32[]{:T(128)}, f32[384,384]{1,0:T(8,128)S(1)}, s32[3,2]{0,1:T(2,128)S(1)}, f32[3,128,128]{2,1,0:T(8,128)}, s32[]{:T(128)}) while((s32[]{:T(128)}, f32[384,384]{1,0:T(8,128)S(1)}, s32[3,2]{0,1:T(2,128)S(1)}, f32[3,128,128]{2,1,0:T(8,128)}, s32[]{:T(128)}) %tuple.129), condition=%wide.while_cond.clone.2, body=%wide.while_body.clone.2.sunk | while | flops 2 | bytes 132705 | solution.py:97
  457.4 31.3 %custom-call.40 = f32[3,128,128]{1,2,0:T(8,128)} custom-call(f32[3,128,128]{2,1,0:T(8,128)} %get-tuple-element.91), custom_call_target="InvertDiagBlocksLowerTriangular" | custom-call | tf_op jit(solution)/shard_map/jit(_solve_triangular)/triangular_solve | solution.py:97
  498.2 11.5 %collective-permute-done.1 = f32[384,384]{0,1:T(8,128)S(1)} collective-permute-done((f32[384,384]{0,1:T(8,128)S(1)}, f32[384,384]{0,1:T(8,128)S(1)}, u32[]{:S(2)}, u32[]{:S(2)}) %collective-permute-start.1) | collective-permute-done | bytes 589856 | tf_op jit(solution)/shard_map/ppermute | solution.py:17
  525.2 21.0 %collective-permute-done.5 = f32[384]{0:T(512)S(1)} collective-permute-done((f32[384]{0:T(512)S(1)}, f32[384]{0:T(512)S(1)}, u32[]{:S(2)}, u32[]{:S(2)}) %collective-permute-start.5) | collective-permute-done | bytes 1568 | tf_op jit(solution)/shard_map/ppermute | solution.py:17
  (293 shorter events, 145.7 us)
Async XLA Ops:
  7.2 10.6 %copy-start.41 = (s32[4,32]{1,0:T(4,128)S(1)}, s32[4,32]{1,0:T(4,128)}, u32[]{:S(2)}) copy-start(s32[4,32]{1,0:T(4,128)} %param.20) | copy-start | bytes 1540
  7.2 10.7 %copy-start.12 = (f32[4,24,4,32]{3,2,1,0:T(4,128)S(1)}, f32[4,24,4,32]{3,2,1,0:T(4,128)}, u32[]{:S(2)}) copy-start(f32[4,24,4,32]{3,2,1,0:T(4,128)} %param.16) | copy-start | bytes 147460
  7.2 118.6 %all-reduce.6.cloned.1.call-start = ((), (), s32[]{:S(2)}) async-start(), calls=%async_computation | async-start | bytes 6684672 | tf_op jit(solution)/shard_map/psum | solution.py:127
  9.1 9.6 %copy-start.7 = (f32[4,3,4,32]{1,0,3,2:T(4,128)}, f32[4,3,4,32]{1,0,3,2:T(4,128)S(1)}, u32[]{:S(2)}) copy-start(f32[4,3,4,32]{1,0,3,2:T(4,128)S(1)} %copy.139) | copy-start | bytes 18436
  29.2 6.2 %copy-start.13 = (f32[4,24,4,32]{3,2,1,0:T(4,128)S(1)}, f32[4,24,4,32]{3,2,1,0:T(4,128)}, u32[]{:S(2)}) copy-start(f32[4,24,4,32]{3,2,1,0:T(4,128)} %param.16) | copy-start | bytes 147460
  29.2 7.0 %copy-start.28 = (s32[67,4,32]{0,2,1:T(8,128)S(1)}, s32[67,4,32]{0,2,1:T(8,128)}, u32[]{:S(2)}) copy-start(s32[67,4,32]{0,2,1:T(8,128)} %copy-done.27) | copy-start | bytes 102916
  64.3 7.5 %collective-permute-start.4 = (f32[18]{0:T(128)S(1)}, f32[18]{0:T(128)S(1)}, u32[]{:S(2)}, u32[]{:S(2)}) collective-permute-start(f32[18]{0:T(128)S(1)} %slice_bitcast_fusion.47), channel_id=1, source_target_pairs={{28,0},{0,4},{4,8},{8,12},{12,16},{16,20},{20,24},{24,28},{29,1},{... | collective-permute-start | bytes 224 | tf_op jit(solution)/shard_map/ppermute | solution.py:17
  126.7 9.9 %collective-permute-start = (f32[18,402]{0,1:T(8,128)S(1)}, f32[18,402]{0,1:T(8,128)S(1)}, u32[]{:S(2)}, u32[]{:S(2)}) collective-permute-start(f32[18,402]{0,1:T(8,128)S(1)} %slice_bitcast_fusion.8), channel_id=1, source_target_pairs={{28,0},{0,4},{4,8},{8,12},{12,16},{16,20},{20,24},{24,28},{29,1},{... | collective-permute-start | bytes 86840 | tf_op jit(solution)/shard_map/ppermute | solution.py:17
  246.1 12.1 %copy-start.33 = (f32[128,1]{0,1:T(1,128)}, f32[128,1]{0,1:T(1,128)S(1)}, u32[]{:S(2)}) copy-start(f32[128,1]{0,1:T(1,128)S(1)} %convolution_bitcast_fusion.21) | copy-start | bytes 1540
  247.2 11.1 %copy-start.37 = (f32[128,1]{0,1:T(1,128)}, f32[128,1]{0,1:T(1,128)S(1)}, u32[]{:S(2)}) copy-start(f32[128,1]{0,1:T(1,128)S(1)} %convolution_bitcast_fusion.19) | copy-start | bytes 1540
  248.2 10.0 %copy-start.43 = (f32[128,1]{0,1:T(1,128)}, f32[128,1]{0,1:T(1,128)S(1)}, u32[]{:S(2)}) copy-start(f32[128,1]{0,1:T(1,128)S(1)} %convolution_bitcast_fusion.17) | copy-start | bytes 1540
  256.1 15.8 %copy-start.23 = (f32[128,384]{1,0:T(8,128)}, f32[128,384]{1,0:T(8,128)S(1)}, u32[]{:S(2)}) copy-start(f32[128,384]{1,0:T(8,128)S(1)} %fusion.69) | copy-start | bytes 589828
  323.1 42.2 %copy-start.42 = (f32[384]{0:T(512)S(1)}, f32[384]{0:T(512)}, u32[]{:S(2)}) copy-start(f32[384]{0:T(512)} %convolution_reduce_fusion.4) | copy-start | bytes 4612
  358.5 6.8 %copy-start.9 = (f32[3,128,128]{1,2,0:T(8,128)}, f32[3,128,128]{1,2,0:T(8,128)S(1)}, u32[]{:S(2)}) copy-start(f32[3,128,128]{1,2,0:T(8,128)S(1)} %custom-call.37) | copy-start | bytes 589828
  358.7 6.6 %copy-start.35 = (f32[128,1]{0,1:T(1,128)}, f32[128,1]{0,1:T(1,128)S(1)}, u32[]{:S(2)}) copy-start(f32[128,1]{0,1:T(1,128)S(1)} %convolution_bitcast_fusion.16) | copy-start | bytes 1540
  359.1 6.2 %copy-start.39 = (f32[128,1]{0,1:T(1,128)}, f32[128,1]{0,1:T(1,128)S(1)}, u32[]{:S(2)}) copy-start(f32[128,1]{0,1:T(1,128)S(1)} %convolution_bitcast_fusion.14) | copy-start | bytes 1540
  488.7 6.6 %copy-start.11 = (f32[3,128,128]{1,2,0:T(8,128)S(1)}, f32[3,128,128]{1,2,0:T(8,128)}, u32[]{:S(2)}) copy-start(f32[3,128,128]{1,2,0:T(8,128)} %custom-call.40) | copy-start | bytes 589828
  488.7 7.0 %copy-start.26 = (f32[384,384]{0,1:T(8,128)S(1)}, f32[384,384]{0,1:T(8,128)}, u32[]{:S(2)}) copy-start(f32[384,384]{0,1:T(8,128)} %get-tuple-element.153) | copy-start | bytes 1769476
  491.0 18.8 %copy-start.10 = (f32[3,128,128]{1,2,0:T(8,128)S(1)}, f32[3,128,128]{1,2,0:T(8,128)}, u32[]{:S(2)}) copy-start(f32[3,128,128]{1,2,0:T(8,128)} %copy-done.9) | copy-start | bytes 589828
  495.2 16.4 %copy-start.5 = (f32[128,384]{1,0:T(8,128)S(1)}, f32[128,384]{1,0:T(8,128)}, u32[]{:S(2)}) copy-start(f32[128,384]{1,0:T(8,128)} %copy-done.4) | copy-start | bytes 589828
  495.2 16.4 %copy-start.18 = (f32[128,384]{1,0:T(8,128)S(1)}, f32[128,384]{1,0:T(8,128)}, u32[]{:S(2)}) copy-start(f32[128,384]{1,0:T(8,128)} %copy-done.17) | copy-start | bytes 589828
  495.3 16.4 %copy-start.25 = (f32[128,384]{1,0:T(8,128)S(1)}, f32[128,384]{1,0:T(8,128)}, u32[]{:S(2)}) copy-start(f32[128,384]{1,0:T(8,128)} %copy-done.24) | copy-start | bytes 589828
  495.7 14.1 %collective-permute-start.1 = (f32[384,384]{0,1:T(8,128)S(1)}, f32[384,384]{0,1:T(8,128)S(1)}, u32[]{:S(2)}, u32[]{:S(2)}) collective-permute-start(f32[384,384]{0,1:T(8,128)S(1)} %copy-done.26), channel_id=1, source_target_pairs={{4,0},{8,4},{12,8},{16,12},{20,16},{24,20},{28,24},{0,28},{5,1},{9... | collective-permute-start | bytes 1769480 | tf_op jit(solution)/shard_map/ppermute | solution.py:17
  515.4 5.1 copy-start.2
  516.2 5.6 %copy-start.34 = (f32[128,1]{0,1:T(1,128)S(1)}, f32[128,1]{0,1:T(1,128)}, u32[]{:S(2)}) copy-start(f32[128,1]{0,1:T(1,128)} %copy-done.33) | copy-start | bytes 1540
  516.2 5.6 %copy-start.38 = (f32[128,1]{0,1:T(1,128)S(1)}, f32[128,1]{0,1:T(1,128)}, u32[]{:S(2)}) copy-start(f32[128,1]{0,1:T(1,128)} %copy-done.37) | copy-start | bytes 1540
  516.2 5.6 %copy-start.44 = (f32[128,1]{0,1:T(1,128)S(1)}, f32[128,1]{0,1:T(1,128)}, u32[]{:S(2)}) copy-start(f32[128,1]{0,1:T(1,128)} %copy-done.43) | copy-start | bytes 1540
  516.2 6.1 %copy-start.36 = (f32[128,1]{0,1:T(1,128)S(1)}, f32[128,1]{0,1:T(1,128)}, u32[]{:S(2)}) copy-start(f32[128,1]{0,1:T(1,128)} %copy-done.35) | copy-start | bytes 1540
  516.2 6.1 %copy-start.40 = (f32[128,1]{0,1:T(1,128)S(1)}, f32[128,1]{0,1:T(1,128)}, u32[]{:S(2)}) copy-start(f32[128,1]{0,1:T(1,128)} %copy-done.39) | copy-start | bytes 1540
  517.5 29.2 %collective-permute-start.2 = (f32[384,384]{0,1:T(8,128)S(1)}, f32[384,384]{0,1:T(8,128)S(1)}, u32[]{:S(2)}, u32[]{:S(2)}) collective-permute-start(f32[384,384]{0,1:T(8,128)S(1)} %convolution_add_fusion), channel_id=1, source_target_pairs={{28,0},{0,4},{4,8},{8,12},{12,16},{16,20},{20,24},{24,28},{29,1},{... | collective-permute-start | bytes 1769480 | tf_op jit(solution)/shard_map/ppermute | solution.py:17
  519.1 30.1 %collective-permute-start.3 = (f32[384,384]{1,0:T(8,128)S(1)}, f32[384,384]{1,0:T(8,128)}, u32[]{:S(2)}, u32[]{:S(2)}) collective-permute-start(f32[384,384]{1,0:T(8,128)S(1)} %fusion.51), channel_id=1, source_target_pairs={{28,0},{0,4},{4,8},{8,12},{12,16},{16,20},{20,24},{24,28},{29,1},{... | collective-permute-start | bytes 1769480 | tf_op jit(solution)/shard_map/ppermute | solution.py:17
  523.2 23.0 %collective-permute-start.5 = (f32[384]{0:T(512)S(1)}, f32[384]{0:T(512)S(1)}, u32[]{:S(2)}, u32[]{:S(2)}) collective-permute-start(f32[384]{0:T(512)S(1)} %add.79), channel_id=1, source_target_pairs={{28,0},{0,4},{4,8},{8,12},{12,16},{16,20},{20,24},{24,28},{29,1},{... | collective-permute-start | bytes 4616 | tf_op jit(solution)/shard_map/ppermute | solution.py:17
  (20 other events, 52.6 us)
Sparse Core Ops, SparseCore 0:
  51.2 74.5 all-reduce.5
where the time goes:
time: 567 us; the launch traced here: 558 us
  other arithmetic  288 us (51%)
  waiting for transfers between devices  92.9 us (16%)
  matrix products  79.7 us (14%)
  local copies, waits for them, and re-layouts  59.1 us (10%)
  between operations  21.1 us (4%)
  blocking collectives  8.76 us (2%)
  starting transfers between devices  8.06 us (1%)
    another operation x33, other arithmetic, eliminate(): factor = jnp.linalg.cholesky(diagonal)  181 us
    another operation x7, other arithmetic, lower_solve(): return jax.scipy.linalg.solve_triangular(factor, right_hand, lower=True)  92.5 us
    psum x1, waiting for transfers between devices, local(): schur_mat, schur_vec = lax.psum((schur_mat, schur_vec), 'lm')  54 us
    ppermute x6, waiting for transfers between devices, passed_along(): return lax.ppermute(block, axis, route)  38.8 us
    another operation x45, matrix products, lower_solve(): return jax.scipy.linalg.solve_triangular(factor, right_hand, lower=True)  23 us
    another operation x31, local copies, waits for them, and re-layouts, lower_solve(): return jax.scipy.linalg.solve_triangular(factor, right_hand, lower=True)  21.2 us
    another operation x12, matrix products, eliminate(): factor = jnp.linalg.cholesky(diagonal)  12.5 us
  transfers between devices with their start and end apart: 7, of which 4 were waited for; matrix products, arithmetic and copies ran while one was open for 4% of the time, Pallas kernels for 0%

commit v1 on v0

--- a/solution.py
+++ b/solution.py
@@ -142,8 +142,16 @@
         cam_rhs - schur_vec[:, :blocks] - jnp.pad(spill_vec, ((0, 0), (0, blocks - border)))
     )
     after_coupling = passed_along(coupling[0], "tm", -1)
-    next_first, prev_first = eliminate((diagonal[1], coupling[1], right_side[1], coupling[2]))
-    next_last, prev_last = eliminate((diagonal[3], coupling[3], right_side[3], after_coupling))
+    pair = jax.vmap(eliminate)(
+        (
+            jnp.stack([diagonal[1], diagonal[3]]),
+            jnp.stack([coupling[1], coupling[3]]),
+            jnp.stack([right_side[1], right_side[3]]),
+            jnp.stack([coupling[2], after_coupling]),
+        )
+    )
+    next_first, prev_first = jax.tree.map(lambda x: x[0], pair)
+    next_last, prev_last = jax.tree.map(lambda x: x[1], pair)
     mid_diag = diagonal[2] - next_first[0] - prev_last[0]
     mid_coupling = -next_first[1]
     mid_rhs = right_side[2] - next_first[2] - prev_last[1]

time: 567 us -> 565 us (level)
  other arithmetic: 288 us -> 299 us
  matrix products: 79.7 us -> 71.5 us
    another operation x45 -> x30, matrix products: 23 us -> 18.7 us  [lower_solve(): return jax.scipy.linalg.solve_triangular(factor, right_hand, lower=True)]
    another operation x7 -> x12, other arithmetic: 92.5 us -> 96.1 us  [lower_solve(): return jax.scipy.linalg.solve_triangular(factor, right_hand, lower=True)]
    another operation x33 -> x25, other arithmetic: 181 us -> 184 us  [eliminate(): factor = jnp.linalg.cholesky(diagonal)]
    another operation x31 -> x21, local copies, waits for them, and re-layouts: 21.2 us -> 18.5 us  [lower_solve(): return jax.scipy.linalg.solve_triangular(factor, right_hand, lower=True)]
    another operation x12 -> x8, matrix products: 12.5 us -> 11.4 us  [eliminate(): factor = jnp.linalg.cholesky(diagonal)]
where the time goes in v1:
time: 565 us; the launch traced here: 557 us
  other arithmetic  299 us (53%)
  waiting for transfers between devices  89.1 us (16%)
  matrix products  71.5 us (13%)
  local copies, waits for them, and re-layouts  63.8 us (11%)
  between operations  16.9 us (3%)
  blocking collectives  8.76 us (2%)
  starting transfers between devices  7.69 us (1%)
    another operation x25, other arithmetic, eliminate(): factor = jnp.linalg.cholesky(diagonal)  184 us
    another operation x12, other arithmetic, lower_solve(): return jax.scipy.linalg.solve_triangular(factor, right_hand, lower=True)  96.1 us
    psum x1, waiting for transfers between devices, local(): schur_mat, schur_vec = lax.psum((schur_mat, schur_vec), 'lm')  52.6 us
    ppermute x6, waiting for transfers between devices, passed_along(): return lax.ppermute(block, axis, route)  36.4 us
    another operation x30, matrix products, lower_solve(): return jax.scipy.linalg.solve_triangular(factor, right_hand, lower=True)  18.7 us
    another operation x21, local copies, waits for them, and re-layouts, lower_solve(): return jax.scipy.linalg.solve_triangular(factor, right_hand, lower=True)  18.5 us
    another operation x8, matrix products, eliminate(): factor = jnp.linalg.cholesky(diagonal)  11.4 us
  transfers between devices with their start and end apart: 7, of which 4 were waited for; matrix products, arithmetic and copies ran while one was open for 4% of the time, Pallas kernels for 0%

profile of v1, /device:TPU:0, one launch (start us, length us, event | category | flops | bytes accessed | tf_op | source)
XLA Modules:
  0.0 557.0 jit_solution(1128424007379267800)
XLA Ops:
  10.9 4.3 subtract_reduce_fusion.7
  19.4 3.2 convolution_bitcast_fusion.1
  22.6 3.8 copy.235
  26.4 2.8 copy.250
  35.3 3.2 convolution_bitcast_fusion
  38.5 3.6 copy.249
  42.1 8.3 %fusion.4 = f32[4,402,402]{1,2,0:T(8,128)} fusion(f32[402,4,4,32]{0,3,1,2:T(8,128)} %copy.250, f32[402,4,4,32]{3,2,1,0:T(4,128)S(1)} %bitcast.332), kind=kOutput, calls=%fused_computation.13 | convolution fusion | flops 992894976 | bytes 4232256 | tf_op jit(solution)/shard_map/while/body/eval_jaxpr/ersl,frsl->sef/dot_general | solution.py:78
  54.9 8.8 %psum.15 = f32[4,402]{1,0:T(4,128)S(1)} all-reduce(f32[4,402]{1,0:T(4,128)S(1)} %bitcast.341), channel_id=1, replica_groups=mesh['tm'=8,'lm'=4] {'lm'}, use_global_device_ids=true, to_apply=%region_13.16 | all-reduce | flops 1608 | bytes 12864 | tf_op jit(solution)/shard_map/psum | solution.py:127
  65.2 3.2 copy.253
  72.5 52.6 %all-reduce.7.cloned.1.call-done = f32[4,402,402]{1,2,0:T(8,128)} async-done(((f32[4,402,402]{1,2,0:T(8,128)}), f32[4,402,402]{1,2,0:T(8,128)}) %all-reduce.7.cloned.1.call-update) | async-done | bytes 2585680 | tf_op jit(solution)/shard_map/psum | solution.py:127
  128.8 6.9 %collective-permute-done = f32[18,402]{0,1:T(8,128)S(1)} collective-permute-done((f32[18,402]{0,1:T(8,128)S(1)}, f32[18,402]{0,1:T(8,128)S(1)}, u32[]{:S(2)}, u32[]{:S(2)}) %collective-permute-start) | collective-permute-done | bytes 28976 | tf_op jit(solution)/shard_map/ppermute | solution.py:17
  135.6 5.0 fusion.3
  147.0 24.5 %custom-call.55 = f32[2,128,128]{2,1,0:T(8,128)} custom-call(f32[2,128,128]{2,1,0:T(8,128)S(1)} %copy.255), custom_call_target="Cholesky" | custom-call | tf_op jit(solution)/shard_map/vmap(jit(cholesky))/cholesky | solution.py:102
  173.2 21.1 %custom-call.56 = f32[2,1,128,128]{2,3,1,0:T(8,128)} custom-call(f32[2,1,128,128]{3,2,1,0:T(8,128)} %select_bitcast_fusion.1), custom_call_target="InvertDiagBlocksLowerTriangular" | custom-call | tf_op jit(solution)/shard_map/vmap(jit(cholesky))/cholesky | solution.py:102
  200.3 24.9 %custom-call.57 = f32[2,128,128]{2,1,0:T(8,128)} custom-call(f32[2,128,128]{2,1,0:T(8,128)} %copy.260), custom_call_target="Cholesky" | custom-call | tf_op jit(solution)/shard_map/vmap(jit(cholesky))/cholesky | solution.py:102
  226.8 21.2 %custom-call.58 = f32[2,1,128,128]{2,3,1,0:T(8,128)} custom-call(f32[2,1,128,128]{3,2,1,0:T(8,128)} %get-tuple-element.138), custom_call_target="InvertDiagBlocksLowerTriangular" | custom-call | tf_op jit(solution)/shard_map/vmap(jit(cholesky))/cholesky | solution.py:102
  253.0 24.9 %custom-call.59 = f32[2,128,128]{2,1,0:T(8,128)} custom-call(f32[2,128,128]{2,1,0:T(8,128)} %copy.265), custom_call_target="Cholesky" | custom-call | tf_op jit(solution)/shard_map/vmap(jit(cholesky))/cholesky | solution.py:102
  281.5 8.3 %while.15 = (s32[]{:T(128)}, f32[2,384,384]{2,1,0:T(8,128)S(1)}, s32[3,2]{0,1:T(2,128)S(1)}, f32[3,2,128,128]{3,2,0,1:T(8,128)}, s32[]{:T(128)}) while((s32[]{:T(128)}, f32[2,384,384]{2,1,0:T(8,128)S(1)}, s32[3,2]{0,1:T(2,128)S(1)}, f32[3,2,128,128]{3,2,0,1:T(8,128)}, s32[]{:T(128)}) %tuple.90), condition=%wide.while_cond, body=%wide.while_body.sunk | while | flops 2 | bytes 263777 | solution.py:97
  289.8 60.5 %custom-call.66 = f32[2,3,128,128]{2,3,1,0:T(8,128)} custom-call(f32[2,3,128,128]{3,2,1,0:T(8,128)} %bitcast.364), custom_call_target="InvertDiagBlocksLowerTriangular" | custom-call | tf_op jit(solution)/shard_map/vmap(jit(_solve_triangular))/triangular_solve | solution.py:97
  365.5 5.0 collective-permute-done.1
  374.2 2.9 fusion.31
  384.2 13.2 %cholesky.338 = f32[128,128]{1,0:T(8,128)} custom-call(f32[128,128]{1,0:T(8,128)} %cholesky.392), custom_call_target="Cholesky" | custom-call | tf_op jit(solution)/shard_map/jit(cholesky)/cholesky | solution.py:102
  400.6 4.7 fusion.30
  405.8 10.6 %custom-call.60 = f32[1,128,128]{1,2,0:T(8,128)S(1)} custom-call(f32[1,128,128]{2,1,0:T(8,128)} %get-tuple-element.146), custom_call_target="InvertDiagBlocksLowerTriangular" | custom-call | tf_op jit(solution)/shard_map/jit(cholesky)/cholesky | solution.py:102
  419.5 11.9 %cholesky.354 = f32[128,128]{1,0:T(8,128)S(1)} custom-call(f32[128,128]{1,0:T(8,128)S(1)} %cholesky.396), custom_call_target="Cholesky" | custom-call | tf_op jit(solution)/shard_map/jit(cholesky)/cholesky | solution.py:102
  433.2 9.8 %custom-call.61 = f32[1,128,128]{1,2,0:T(8,128)S(1)} custom-call(f32[1,128,128]{2,1,0:T(8,128)S(1)} %get-tuple-element.143), custom_call_target="InvertDiagBlocksLowerTriangular" | custom-call | tf_op jit(solution)/shard_map/jit(cholesky)/cholesky | solution.py:102
  445.1 12.3 %cholesky.373 = f32[128,128]{1,0:T(8,128)} custom-call(f32[128,128]{1,0:T(8,128)S(1)} %convolution_subtract_fusion.7), custom_call_target="Cholesky" | custom-call | tf_op jit(solution)/shard_map/jit(cholesky)/cholesky | solution.py:102
  463.4 10.4 %while.16 = (s32[]{:T(128)}, f32[384,384]{1,0:T(8,128)}, s32[3,2]{0,1:T(2,128)S(1)}, f32[3,128,128]{2,1,0:T(8,128)}, s32[]{:T(128)}) while((s32[]{:T(128)}, f32[384,384]{1,0:T(8,128)}, s32[3,2]{0,1:T(2,128)S(1)}, f32[3,128,128]{2,1,0:T(8,128)}, s32[]{:T(128)}) %tuple.98), condition=%wide.while_cond.1, body=%wide.while_body.1.sunk | while | flops 2 | bytes 132705 | solution.py:97
  464.2 2.8 bitcast_dynamic-update-slice_fusion.5
  467.6 2.8 bitcast_dynamic-update-slice_fusion.5
  473.7 30.9 %custom-call.68 = f32[3,128,128]{1,2,0:T(8,128)} custom-call(f32[3,128,128]{2,1,0:T(8,128)} %get-tuple-element.75), custom_call_target="InvertDiagBlocksLowerTriangular" | custom-call | tf_op jit(solution)/shard_map/jit(_solve_triangular)/triangular_solve | solution.py:97
  520.5 24.5 %collective-permute-done.5 = f32[384]{0:T(512)S(1)} collective-permute-done((f32[384]{0:T(512)S(1)}, f32[384]{0:T(512)S(1)}, u32[]{:S(2)}, u32[]{:S(2)}) %collective-permute-start.5) | collective-permute-done | bytes 1568 | tf_op jit(solution)/shard_map/ppermute | solution.py:17
  (242 shorter events, 125.6 us)
Async XLA Ops:
  7.2 118.0 %all-reduce.7.cloned.1.call-start = ((), (), s32[]{:S(2)}) async-start(), calls=%async_computation | async-start | bytes 6684672 | tf_op jit(solution)/shard_map/psum | solution.py:127
  9.1 7.9 %copy-start.15 = (f32[4,3,4,32]{1,0,3,2:T(4,128)}, f32[4,3,4,32]{1,0,3,2:T(4,128)S(1)}, u32[]{:S(2)}) copy-start(f32[4,3,4,32]{1,0,3,2:T(4,128)S(1)} %copy.239) | copy-start | bytes 18436
  9.1 8.7 %copy-start.34 = (s32[4,32]{1,0:T(4,128)S(1)}, s32[4,32]{1,0:T(4,128)}, u32[]{:S(2)}) copy-start(s32[4,32]{1,0:T(4,128)} %param.19) | copy-start | bytes 1540
  9.1 8.8 %copy-start.19 = (f32[4,24,4,32]{3,2,1,0:T(4,128)S(1)}, f32[4,24,4,32]{3,2,1,0:T(4,128)}, u32[]{:S(2)}) copy-start(f32[4,24,4,32]{3,2,1,0:T(4,128)} %param.15) | copy-start | bytes 147460
  29.1 4.2 copy-start.16
  31.1 3.3 copy-start.20
  50.4 1.8 copy-start.24
  50.4 3.8 copy-start
  63.6 8.8 %collective-permute-start.4 = (f32[18]{0:T(128)S(1)}, f32[18]{0:T(128)S(1)}, u32[]{:S(2)}, u32[]{:S(2)}) collective-permute-start(f32[18]{0:T(128)S(1)} %slice_bitcast_fusion.31), channel_id=1, source_target_pairs={{28,0},{0,4},{4,8},{8,12},{12,16},{16,20},{20,24},{24,28},{29,1},{... | collective-permute-start | bytes 224 | tf_op jit(solution)/shard_map/ppermute | solution.py:17
  65.2 3.2 copy-start.17
  68.5 4.0 copy-start.33
  72.5 68.2 %copy-start.29 = (f32[4,384]{1,0:T(4,128)}, f32[4,384]{1,0:T(4,128)S(1)}, u32[]{:S(2)}) copy-start(f32[4,384]{1,0:T(4,128)S(1)} %fusion.106) | copy-start | bytes 18436
  126.1 9.5 %collective-permute-start = (f32[18,402]{0,1:T(8,128)S(1)}, f32[18,402]{0,1:T(8,128)S(1)}, u32[]{:S(2)}, u32[]{:S(2)}) collective-permute-start(f32[18,402]{0,1:T(8,128)S(1)} %slice_bitcast_fusion.2), channel_id=1, source_target_pairs={{28,0},{0,4},{4,8},{8,12},{12,16},{16,20},{20,24},{24,28},{29,1},{... | collective-permute-start | bytes 86840 | tf_op jit(solution)/shard_map/ppermute | solution.py:17
  127.6 13.0 %copy-start.31 = (f32[2,384,1]{1,0,2:T(2,128)}, f32[2,384,1]{1,0,2:T(2,128)S(1)}, u32[]{:S(2)}) copy-start(f32[2,384,1]{1,0,2:T(2,128)S(1)} %maximum_bitcast_fusion.4) | copy-start | bytes 9220
  226.8 51.1 %copy-start.27 = (pred[128,128]{1,0:T(8,128)(4,1)S(1)}, pred[128,128]{1,0:T(8,128)(4,1)}, u32[]{:S(2)}) copy-start(pred[128,128]{1,0:T(8,128)(4,1)} %iota_compare_fusion.5) | copy-start | bytes 49156
  281.5 68.8 %slice-start = ((f32[2,384,1]{1,0,2:T(2,128)}), f32[2,128,1]{1,0,2:T(2,128)S(1)}, s32[]{:S(2)}) async-start(f32[2,384,1]{1,0,2:T(2,128)} %copy-done.31), calls=%async_computation.1 | async-start | bytes 2048 | tf_op jit(solution)/shard_map/vmap(jit(_solve_triangular))/triangular_solve | solution.py:97
  281.5 70.2 %copy-start.32 = (f32[2,384,1]{1,0,2:T(2,128)S(1)}, f32[2,384,1]{1,0,2:T(2,128)}, u32[]{:S(2)}) copy-start(f32[2,384,1]{1,0,2:T(2,128)} %copy-done.31) | copy-start | bytes 9220
  289.8 66.4 %copy-start.1 = (f32[2,384,384]{2,1,0:T(8,128)}, f32[2,384,384]{2,1,0:T(8,128)S(1)}, u32[]{:S(2)}) copy-start(f32[2,384,384]{2,1,0:T(8,128)S(1)} %get-tuple-element.249) | copy-start | bytes 3538948
  354.4 3.7 copy-start.12
  356.2 2.5 copy-start.2
  356.2 14.3 %collective-permute-start.1 = (f32[384,384]{0,1:T(8,128)S(1)}, f32[384,384]{0,1:T(8,128)S(1)}, u32[]{:S(2)}, u32[]{:S(2)}) collective-permute-start(f32[384,384]{0,1:T(8,128)S(1)} %get-tuple-element.124), channel_id=1, source_target_pairs={{4,0},{8,4},{12,8},{16,12},{20,16},{24,20},{28,24},{0,28},{5,1},{9... | collective-permute-start | bytes 1769480 | tf_op jit(solution)/shard_map/ppermute | solution.py:17
  362.2 3.3 copy-start.11
  365.5 11.7 %copy-start.5 = (f32[2,384,384]{1,2,0:T(8,128)}, f32[2,384,384]{1,2,0:T(8,128)S(1)}, u32[]{:S(2)}) copy-start(f32[2,384,384]{1,2,0:T(8,128)S(1)} %fusion.33) | copy-start | bytes 3538948
  372.2 2.0 copy-start.7
  373.4 3.7 copy-start.13
  443.9 60.8 %copy-start.30 = (f32[4,384]{1,0:T(4,128)S(1)}, f32[4,384]{1,0:T(4,128)}, u32[]{:S(2)}) copy-start(f32[4,384]{1,0:T(4,128)} %copy-done.29) | copy-start | bytes 18436
  457.5 51.0 %copy-start.9 = (f32[2,384,384]{2,1,0:T(8,128)S(1)}, f32[2,384,384]{2,1,0:T(8,128)}, u32[]{:S(2)}) copy-start(f32[2,384,384]{2,1,0:T(8,128)} %fusion.30) | copy-start | bytes 3538948
  511.7 2.1 copy-start.4
  516.5 29.1 %copy-start.6 = (f32[2,384,384]{1,2,0:T(8,128)S(1)}, f32[2,384,384]{1,2,0:T(8,128)}, u32[]{:S(2)}) copy-start(f32[2,384,384]{1,2,0:T(8,128)} %copy-done.5) | copy-start | bytes 3538948
  516.5 31.5 %collective-permute-start.3 = (f32[384,384]{1,0:T(8,128)S(1)}, f32[384,384]{1,0:T(8,128)}, u32[]{:S(2)}, u32[]{:S(2)}) collective-permute-start(f32[384,384]{1,0:T(8,128)S(1)} %fusion.59), channel_id=1, source_target_pairs={{28,0},{0,4},{4,8},{8,12},{12,16},{16,20},{20,24},{24,28},{29,1},{... | collective-permute-start | bytes 1769480 | tf_op jit(solution)/shard_map/ppermute | solution.py:17
  516.5 29.1 %collective-permute-start.2 = (f32[384,384]{0,1:T(8,128)S(1)}, f32[384,384]{0,1:T(8,128)S(1)}, u32[]{:S(2)}, u32[]{:S(2)}) collective-permute-start(f32[384,384]{0,1:T(8,128)S(1)} %convolution_add_fusion), channel_id=1, source_target_pairs={{28,0},{0,4},{4,8},{8,12},{12,16},{16,20},{20,24},{24,28},{29,1},{... | collective-permute-start | bytes 1769480 | tf_op jit(solution)/shard_map/ppermute | solution.py:17
  518.6 26.5 %collective-permute-start.5 = (f32[384]{0:T(512)S(1)}, f32[384]{0:T(512)S(1)}, u32[]{:S(2)}, u32[]{:S(2)}) collective-permute-start(f32[384]{0:T(512)S(1)} %add.122), channel_id=1, source_target_pairs={{28,0},{0,4},{4,8},{8,12},{12,16},{16,20},{20,24},{24,28},{29,1},{... | collective-permute-start | bytes 4616 | tf_op jit(solution)/shard_map/ppermute | solution.py:17
  (12 other events, 12.5 us)
Sparse Core Ops, SparseCore 0:
  50.5 74.5 all-reduce.6

commit v2 on v1

--- a/solution.py
+++ b/solution.py
@@ -100,9 +100,10 @@
 def eliminate(operands):
     diagonal, coupling, right_side, next_coupling = operands
     factor = jnp.linalg.cholesky(diagonal)
-    left_part = lower_solve(factor, coupling)
-    right_part = lower_solve(factor, next_coupling.T)
-    solved_rhs = lower_solve(factor, right_side[:, None])[:, 0]
+    inverse = lower_solve(factor, jnp.eye(diagonal.shape[0], dtype=diagonal.dtype))
+    left_part = jnp.dot(inverse, coupling, precision=PRECISE)
+    right_part = jnp.dot(inverse, next_coupling.T, precision=PRECISE)
+    solved_rhs = jnp.dot(inverse, right_side, precision=PRECISE)
     to_next = (
         jnp.dot(right_part.T, right_part, precision=PRECISE),
         jnp.dot(right_part.T, left_part, precision=PRECISE),
@@ -155,12 +156,11 @@
     mid_diag = diagonal[2] - next_first[0] - prev_last[0]
     mid_coupling = -next_first[1]
     mid_rhs = right_side[2] - next_first[2] - prev_last[1]
+    arrived_last = passed_along((next_last[0], next_last[2]), "tm", 1)
     next_mid, prev_mid = eliminate((mid_diag, mid_coupling, mid_rhs, -next_last[1]))
-    head_diag = diagonal[0] - prev_first[0] - prev_mid[0]
-    head_rhs = right_side[0] - prev_first[1] - prev_mid[1]
-    arrived = passed_along(
-        (next_last[0] + next_mid[0], next_mid[1], next_last[2] + next_mid[2]), "tm", 1
-    )
+    head_diag = diagonal[0] - prev_first[0] - prev_mid[0] - arrived_last[0]
+    head_rhs = right_side[0] - prev_first[1] - prev_mid[1] - arrived_last[1]
+    arrived = passed_along((next_mid[0], next_mid[1], next_mid[2]), "tm", 1)
     out_diag = head_diag - arrived[0]
     out_coupling = -arrived[1]
     out_rhs = head_rhs - arrived[2]

time: 565 us -> 572 us (1.012)
  waiting for transfers between devices: 89.1 us -> 102 us
    another operation x0 -> x18, local copies, waits for them, and re-layouts: none -> 18.5 us
    another operation x21 -> x2, local copies, waits for them, and re-layouts: 18.5 us -> 0.84 us  [lower_solve(): return jax.scipy.linalg.solve_triangular(factor, right_hand, lower=True)]
    another operation x30 -> x10, matrix products: 18.7 us -> 7.1 us  [lower_solve(): return jax.scipy.linalg.solve_triangular(factor, right_hand, lower=True)]
    dot_general x0 -> x6, matrix products: none -> 9.18 us  [the longest x2 3.77 us: eliminate(): left_part = jnp.dot(inverse, coupling, precision=PRECISE)]
    psum x1, waiting for transfers between devices: 52.6 us -> 59.6 us  [local(): schur_mat, schur_vec = lax.psum((schur_mat, schur_vec), 'lm')]
    ppermute x6 -> x8, waiting for transfers between devices: 36.4 us -> 42.6 us  [passed_along(): return lax.ppermute(block, axis, route)]
    another operation x12 -> x6, other arithmetic: 96.1 us -> 94.6 us  [lower_solve(): return jax.scipy.linalg.solve_triangular(factor, right_hand, lower=True)]
  transfers between devices with their start and end apart: 7 -> 9, of which waited for: 4 -> 6; matrix products, arithmetic and copies ran while one was open for 4% -> 8% of each run, Pallas kernels for 0% -> 0%
where the time goes in v2:
time: 572 us; the launch traced here: 562 us
  other arithmetic  295 us (52%)
  waiting for transfers between devices  102 us (18%)
  matrix products  66.6 us (12%)
  local copies, waits for them, and re-layouts  60.6 us (11%)
  between operations  17.2 us (3%)
  starting transfers between devices  11.2 us (2%)
  blocking collectives  8.5 us (1%)
    another operation x25, other arithmetic, eliminate(): factor = jnp.linalg.cholesky(diagonal)  181 us
    another operation x6, other arithmetic, lower_solve(): return jax.scipy.linalg.solve_triangular(factor, right_hand, lower=True)  94.6 us
    psum x1, waiting for transfers between devices, local(): schur_mat, schur_vec = lax.psum((schur_mat, schur_vec), 'lm')  59.6 us
    ppermute x8, waiting for transfers between devices, passed_along(): return lax.ppermute(block, axis, route)  42.6 us
    another operation x18, local copies, waits for them, and re-layouts  18.5 us
  transfers between devices with their start and end apart: 9, of which 6 were waited for; matrix products, arithmetic and copies ran while one was open for 8% of the time, Pallas kernels for 0%

profile of v2, /device:TPU:0, one launch (start us, length us, event | category | flops | bytes accessed | tf_op | source)
XLA Modules:
  0.0 561.6 jit_solution(11028868361358890387)
XLA Ops:
  10.8 4.3 subtract_reduce_fusion.7
  21.6 3.2 convolution_bitcast_fusion.1
  24.7 3.8 copy.201
  33.3 8.5 %psum.15 = f32[4,402]{1,0:T(4,128)S(1)} all-reduce(f32[4,402]{1,0:T(4,128)S(1)} %bitcast.252), channel_id=1, replica_groups=mesh['tm'=8,'lm'=4] {'lm'}, use_global_device_ids=true, to_apply=%region_13.14 | all-reduce | flops 1608 | bytes 12864 | tf_op jit(solution)/shard_map/psum | solution.py:128
  48.2 3.2 convolution_bitcast_fusion
  51.4 3.6 copy.215
  55.0 8.1 %fusion.4 = f32[4,402,402]{1,2,0:T(8,128)} fusion(f32[402,4,4,32]{0,3,1,2:T(8,128)} %copy.216, f32[402,4,4,32]{3,2,1,0:T(4,128)S(1)} %bitcast.243), kind=kOutput, calls=%fused_computation.13 | convolution fusion | flops 992894976 | bytes 4232256 | tf_op jit(solution)/shard_map/while/body/eval_jaxpr/ersl,frsl->sef/dot_general | solution.py:78
  66.8 3.5 copy.236
  74.7 59.6 %all-reduce.7.cloned.1.call-done = f32[4,402,402]{1,2,0:T(8,128)} async-done(((f32[4,402,402]{1,2,0:T(8,128)}), f32[4,402,402]{1,2,0:T(8,128)}) %all-reduce.7.cloned.1.call-update) | async-done | bytes 2585680 | tf_op jit(solution)/shard_map/psum | solution.py:128
  138.9 6.3 %collective-permute-done = f32[18,402]{0,1:T(8,128)S(1)} collective-permute-done((f32[18,402]{0,1:T(8,128)S(1)}, f32[18,402]{0,1:T(8,128)S(1)}, u32[]{:S(2)}, u32[]{:S(2)}) %collective-permute-start) | collective-permute-done | bytes 28976 | tf_op jit(solution)/shard_map/ppermute | solution.py:17
  145.2 3.6 fusion.3
  156.5 24.1 %custom-call.49 = f32[2,128,128]{2,1,0:T(8,128)} custom-call(f32[2,128,128]{2,1,0:T(8,128)S(1)} %copy.221), custom_call_target="Cholesky" | custom-call | tf_op jit(solution)/shard_map/vmap(jit(cholesky))/cholesky | solution.py:102
  182.3 21.1 %custom-call.50 = f32[2,1,128,128]{2,3,1,0:T(8,128)} custom-call(f32[2,1,128,128]{3,2,1,0:T(8,128)} %select_bitcast_fusion.1), custom_call_target="InvertDiagBlocksLowerTriangular" | custom-call | tf_op jit(solution)/shard_map/vmap(jit(cholesky))/cholesky | solution.py:102
  209.3 24.9 %custom-call.51 = f32[2,128,128]{2,1,0:T(8,128)} custom-call(f32[2,128,128]{2,1,0:T(8,128)} %copy.226), custom_call_target="Cholesky" | custom-call | tf_op jit(solution)/shard_map/vmap(jit(cholesky))/cholesky | solution.py:102
  235.8 21.3 %custom-call.52 = f32[2,1,128,128]{2,3,1,0:T(8,128)} custom-call(f32[2,1,128,128]{3,2,1,0:T(8,128)} %get-tuple-element.107), custom_call_target="InvertDiagBlocksLowerTriangular" | custom-call | tf_op jit(solution)/shard_map/vmap(jit(cholesky))/cholesky | solution.py:102
  262.0 24.9 %custom-call.53 = f32[2,128,128]{2,1,0:T(8,128)} custom-call(f32[2,128,128]{2,1,0:T(8,128)} %copy.231), custom_call_target="Cholesky" | custom-call | tf_op jit(solution)/shard_map/vmap(jit(cholesky))/cholesky | solution.py:102
  290.5 10.8 %while.2 = (s32[]{:T(128)}, f32[2,384,384]{2,1,0:T(8,128)}, s32[3,2]{0,1:T(2,128)S(1)}, f32[3,2,128,128]{3,2,0,1:T(8,128)}, s32[]{:T(128)}) while((s32[]{:T(128)}, f32[2,384,384]{2,1,0:T(8,128)}, s32[3,2]{0,1:T(2,128)S(1)}, f32[3,2,128,128]{3,2,0,1:T(8,128)}, s32[]{:T(128)}) %tuple.74), condition=%wide.while_cond, body=%wide.while_body.sunk | while | flops 2 | bytes 263777 | solution.py:97
  291.1 3.0 bitcast_dynamic-update-slice_fusion.4
  294.8 3.0 bitcast_dynamic-update-slice_fusion.4
  298.4 2.9 bitcast_dynamic-update-slice_fusion.4
  301.3 59.8 %custom-call.54 = f32[2,3,128,128]{2,3,1,0:T(8,128)S(1)} custom-call(f32[2,3,128,128]{3,2,1,0:T(8,128)} %bitcast.268), custom_call_target="InvertDiagBlocksLowerTriangular" | custom-call | tf_op jit(solution)/shard_map/vmap(jit(_solve_triangular))/triangular_solve | solution.py:97
  375.6 6.1 %collective-permute-done.1 = f32[384,384]{0,1:T(8,128)S(1)} collective-permute-done((f32[384,384]{0,1:T(8,128)S(1)}, f32[384,384]{0,1:T(8,128)S(1)}, u32[]{:S(2)}, u32[]{:S(2)}) %collective-permute-start.1) | collective-permute-done | bytes 589856 | tf_op jit(solution)/shard_map/ppermute | solution.py:17
  394.0 11.9 %cholesky.338 = f32[128,128]{1,0:T(8,128)S(1)} custom-call(f32[128,128]{1,0:T(8,128)S(1)} %cholesky.392), custom_call_target="Cholesky" | custom-call | tf_op jit(solution)/shard_map/jit(cholesky)/cholesky | solution.py:102
  410.3 10.6 %custom-call.55 = f32[1,128,128]{1,2,0:T(8,128)S(1)} custom-call(f32[1,128,128]{2,1,0:T(8,128)} %get-tuple-element.115), custom_call_target="InvertDiagBlocksLowerTriangular" | custom-call | tf_op jit(solution)/shard_map/jit(cholesky)/cholesky | solution.py:102
  424.0 11.9 %cholesky.354 = f32[128,128]{1,0:T(8,128)S(1)} custom-call(f32[128,128]{1,0:T(8,128)S(1)} %cholesky.396), custom_call_target="Cholesky" | custom-call | tf_op jit(solution)/shard_map/jit(cholesky)/cholesky | solution.py:102
  437.8 9.8 %custom-call.56 = f32[1,128,128]{1,2,0:T(8,128)S(1)} custom-call(f32[1,128,128]{2,1,0:T(8,128)S(1)} %get-tuple-element.112), custom_call_target="InvertDiagBlocksLowerTriangular" | custom-call | tf_op jit(solution)/shard_map/jit(cholesky)/cholesky | solution.py:102
  449.7 11.7 %cholesky.373 = f32[128,128]{1,0:T(8,128)S(1)} custom-call(f32[128,128]{1,0:T(8,128)S(1)} %convolution_subtract_fusion.7), custom_call_target="Cholesky" | custom-call | tf_op jit(solution)/shard_map/jit(cholesky)/cholesky | solution.py:102
  465.7 8.0 %while.3 = (s32[]{:T(128)}, f32[384,384]{1,0:T(8,128)S(1)}, s32[3,2]{0,1:T(2,128)S(1)}, f32[3,128,128]{2,1,0:T(8,128)}, s32[]{:T(128)}) while((s32[]{:T(128)}, f32[384,384]{1,0:T(8,128)S(1)}, s32[3,2]{0,1:T(2,128)S(1)}, f32[3,128,128]{2,1,0:T(8,128)}, s32[]{:T(128)}) %tuple.82), condition=%wide.while_cond.1, body=%wide.while_body.1.sunk | while | flops 2 | bytes 132705 | solution.py:97
  473.7 30.3 %custom-call.57 = f32[3,128,128]{1,2,0:T(8,128)S(1)} custom-call(f32[3,128,128]{2,1,0:T(8,128)} %get-tuple-element.42), custom_call_target="InvertDiagBlocksLowerTriangular" | custom-call | tf_op jit(solution)/shard_map/jit(_solve_triangular)/triangular_solve | solution.py:97
  519.7 12.1 %collective-permute-done.3 = f32[384,384]{0,1:T(8,128)S(1)} collective-permute-done((f32[384,384]{0,1:T(8,128)S(1)}, f32[384,384]{0,1:T(8,128)S(1)}, u32[]{:S(2)}, u32[]{:S(2)}) %collective-permute-start.3) | collective-permute-done | bytes 589856 | tf_op jit(solution)/shard_map/ppermute | solution.py:17
  531.8 12.6 %collective-permute-done.2 = f32[384,384]{0,1:T(8,128)S(1)} collective-permute-done((f32[384,384]{0,1:T(8,128)S(1)}, f32[384,384]{0,1:T(8,128)S(1)}, u32[]{:S(2)}, u32[]{:S(2)}) %collective-permute-start.2) | collective-permute-done | bytes 589856 | tf_op jit(solution)/shard_map/ppermute | solution.py:17
  548.0 5.5 collective-permute-done.4
  (228 shorter events, 129.2 us)
Async XLA Ops:
  7.2 127.1 %all-reduce.7.cloned.1.call-start = ((), (), s32[]{:S(2)}) async-start(), calls=%async_computation | async-start | bytes 6684672 | tf_op jit(solution)/shard_map/psum | solution.py:128
  8.1 11.0 %copy-start.6 = (f32[4,3,4,32]{0,1,3,2:T(4,128)}, f32[4,3,4,32]{0,1,3,2:T(4,128)S(1)}, u32[]{:S(2)}) copy-start(f32[4,3,4,32]{0,1,3,2:T(4,128)S(1)} %copy.203) | copy-start | bytes 18436
  9.1 7.9 %copy-start.23 = (f32[4,4,32]{2,1,0:T(4,128)S(1)}, f32[4,4,32]{2,1,0:T(4,128)}, u32[]{:S(2)}) copy-start(f32[4,4,32]{2,1,0:T(4,128)} %param.13) | copy-start | bytes 6148
  16.3 4.4 copy-start.33
  16.3 4.5 copy-start.9
  17.0 3.8 copy-start.14
  31.3 12.6 %copy-start.10 = (f32[4,24,4,32]{3,2,1,0:T(4,128)S(1)}, f32[4,24,4,32]{3,2,1,0:T(4,128)}, u32[]{:S(2)}) copy-start(f32[4,24,4,32]{3,2,1,0:T(4,128)} %param.11) | copy-start | bytes 147460
  31.3 12.7 %copy-start.7 = (f32[4,3,4,32]{0,1,3,2:T(4,128)S(1)}, f32[4,3,4,32]{0,1,3,2:T(4,128)}, u32[]{:S(2)}) copy-start(f32[4,3,4,32]{0,1,3,2:T(4,128)} %copy-done.6) | copy-start | bytes 18436
  31.3 13.7 %copy-start.15 = (f32[3,3,4,32]{0,1,3,2:T(4,128)S(1)}, f32[3,3,4,32]{0,1,3,2:T(4,128)}, u32[]{:S(2)}) copy-start(f32[3,3,4,32]{0,1,3,2:T(4,128)} %copy-done.14) | copy-start | bytes 13828
  41.8 2.1 copy-start.24
  42.4 31.7 %collective-permute-start.5 = (f32[18]{0:T(128)}, f32[18]{0:T(128)}, u32[]{:S(2)}, u32[]{:S(2)}) collective-permute-start(f32[18]{0:T(128)} %slice_bitcast_fusion.15), channel_id=1, source_target_pairs={{28,0},{0,4},{4,8},{8,12},{12,16},{16,20},{20,24},{24,28},{29,1},{... | collective-permute-start | bytes 224 | tf_op jit(solution)/shard_map/ppermute | solution.py:17
  70.3 3.8 copy-start.31
  74.7 74.1 %copy-start.26 = (f32[4,384]{1,0:T(4,128)}, f32[4,384]{1,0:T(4,128)S(1)}, u32[]{:S(2)}) copy-start(f32[4,384]{1,0:T(4,128)S(1)} %fusion.72) | copy-start | bytes 18436
  135.2 10.0 %collective-permute-start = (f32[18,402]{0,1:T(8,128)S(1)}, f32[18,402]{0,1:T(8,128)S(1)}, u32[]{:S(2)}, u32[]{:S(2)}) collective-permute-start(f32[18,402]{0,1:T(8,128)S(1)} %slice_bitcast_fusion.2), channel_id=1, source_target_pairs={{28,0},{0,4},{4,8},{8,12},{12,16},{16,20},{20,24},{24,28},{29,1},{... | collective-permute-start | bytes 86840 | tf_op jit(solution)/shard_map/ppermute | solution.py:17
  235.8 51.1 %copy-start.22 = (pred[128,128]{1,0:T(8,128)(4,1)S(1)}, pred[128,128]{1,0:T(8,128)(4,1)}, u32[]{:S(2)}) copy-start(pred[128,128]{1,0:T(8,128)(4,1)} %iota_compare_fusion.6) | copy-start | bytes 49156
  288.3 2.2 copy-start.35
  290.5 70.6 %copy-start.17 = (f32[128,384]{1,0:T(8,128)S(1)}, f32[128,384]{1,0:T(8,128)}, u32[]{:S(2)}) copy-start(f32[128,384]{1,0:T(8,128)} %get-tuple-element.101) | copy-start | bytes 589828
  290.5 71.1 %copy-start.18 = (f32[128,384]{1,0:T(8,128)S(1)}, f32[128,384]{1,0:T(8,128)}, u32[]{:S(2)}) copy-start(f32[128,384]{1,0:T(8,128)} %get-tuple-element.100) | copy-start | bytes 589828
  363.6 2.2 copy-start.32
  367.2 14.5 %collective-permute-start.1 = (f32[384,384]{0,1:T(8,128)S(1)}, f32[384,384]{0,1:T(8,128)S(1)}, u32[]{:S(2)}, u32[]{:S(2)}) collective-permute-start(f32[384,384]{0,1:T(8,128)S(1)} %get-tuple-element.90), channel_id=1, source_target_pairs={{4,0},{8,4},{12,8},{16,12},{20,16},{24,20},{28,24},{0,28},{5,1},{9... | collective-permute-start | bytes 1769480 | tf_op jit(solution)/shard_map/ppermute | solution.py:17
  372.5 3.1 copy-start.29
  375.6 11.6 %copy-start.1 = (f32[2,384,384]{1,2,0:T(8,128)}, f32[2,384,384]{1,2,0:T(8,128)S(1)}, u32[]{:S(2)}) copy-start(f32[2,384,384]{1,2,0:T(8,128)S(1)} %fusion.99) | copy-start | bytes 3538948
  410.3 26.9 %copy-start.34 = (f32[128]{0:T(128)S(1)}, f32[128]{0:T(128)}, u32[]{:S(2)}) copy-start(f32[128]{0:T(128)} %get-tuple-element.114) | copy-start | bytes 1540
  462.1 43.0 %copy-start.4 = (f32[384,384]{1,0:T(8,128)S(1)}, f32[384,384]{1,0:T(8,128)}, u32[]{:S(2)}) copy-start(f32[384,384]{1,0:T(8,128)} %copy-done.3) | copy-start | bytes 1769476
  509.8 4.5 copy-start.19
  511.7 7.5 %collective-permute-start.7 = (f32[384]{0:T(512)S(1)}, f32[384]{0:T(512)S(1)}, u32[]{:S(2)}, u32[]{:S(2)}) collective-permute-start(f32[384]{0:T(512)S(1)} %convolution_reduce_fusion), channel_id=1, source_target_pairs={{28,0},{0,4},{4,8},{8,12},{12,16},{16,20},{20,24},{24,28},{29,1},{... | collective-permute-start | bytes 4616 | tf_op jit(solution)/shard_map/ppermute | solution.py:17
  511.7 7.4 %collective-permute-start.6 = (f32[384]{0:T(512)S(1)}, f32[384]{0:T(512)S(1)}, u32[]{:S(2)}, u32[]{:S(2)}) collective-permute-start(f32[384]{0:T(512)S(1)} %slice_reduce_fusion), channel_id=1, source_target_pairs={{28,0},{0,4},{4,8},{8,12},{12,16},{16,20},{20,24},{24,28},{29,1},{... | collective-permute-start | bytes 4616 | tf_op jit(solution)/shard_map/ppermute | solution.py:17
  512.9 19.0 %collective-permute-start.3 = (f32[384,384]{0,1:T(8,128)S(1)}, f32[384,384]{0,1:T(8,128)S(1)}, u32[]{:S(2)}, u32[]{:S(2)}) collective-permute-start(f32[384,384]{0,1:T(8,128)S(1)} %fusion.102), channel_id=1, source_target_pairs={{28,0},{0,4},{4,8},{8,12},{12,16},{16,20},{20,24},{24,28},{29,1},{... | collective-permute-start | bytes 1769480 | tf_op jit(solution)/shard_map/ppermute | solution.py:17
  514.3 4.8 copy-start.28
  514.3 30.1 %copy-start.2 = (f32[2,384,384]{1,2,0:T(8,128)S(1)}, f32[2,384,384]{1,2,0:T(8,128)}, u32[]{:S(2)}) copy-start(f32[2,384,384]{1,2,0:T(8,128)} %copy-done.1) | copy-start | bytes 3538948
  514.3 30.1 %collective-permute-start.2 = (f32[384,384]{0,1:T(8,128)S(1)}, f32[384,384]{0,1:T(8,128)S(1)}, u32[]{:S(2)}, u32[]{:S(2)}) collective-permute-start(f32[384,384]{0,1:T(8,128)S(1)} %copy-done.19), channel_id=1, source_target_pairs={{28,0},{0,4},{4,8},{8,12},{12,16},{16,20},{20,24},{24,28},{29,1},{... | collective-permute-start | bytes 1769480 | tf_op jit(solution)/shard_map/ppermute | solution.py:17
  517.1 36.3 %collective-permute-start.4 = (f32[384,384]{1,0:T(8,128)S(1)}, f32[384,384]{1,0:T(8,128)S(1)}, u32[]{:S(2)}, u32[]{:S(2)}) collective-permute-start(f32[384,384]{1,0:T(8,128)S(1)} %fusion.103), channel_id=1, source_target_pairs={{28,0},{0,4},{4,8},{8,12},{12,16},{16,20},{20,24},{24,28},{29,1},{... | collective-permute-start | bytes 1769480 | tf_op jit(solution)/shard_map/ppermute | solution.py:17
  (13 other events, 13.8 us)
Sparse Core Ops, SparseCore 0:
  63.2 70.9 all-reduce.6

commit v3 on v2

--- a/solution.py
+++ b/solution.py
@@ -2,6 +2,8 @@
 import jax.numpy as jnp
 from jax import lax
 from jax.sharding import PartitionSpec as P
+from jax.experimental import pallas as pl
+from jax.experimental.pallas import tpu as pltpu
 
 KNOTS = 64
 DOF = 6
@@ -93,25 +95,69 @@
     return totals
 
 
-def lower_solve(factor, right_hand):
-    return jax.scipy.linalg.solve_triangular(factor, right_hand, lower=True)
-
-
-def eliminate(operands):
-    diagonal, coupling, right_side, next_coupling = operands
-    factor = jnp.linalg.cholesky(diagonal)
-    inverse = lower_solve(factor, jnp.eye(diagonal.shape[0], dtype=diagonal.dtype))
-    left_part = jnp.dot(inverse, coupling, precision=PRECISE)
-    right_part = jnp.dot(inverse, next_coupling.T, precision=PRECISE)
-    solved_rhs = jnp.dot(inverse, right_side, precision=PRECISE)
+PIVOT = 128
+
+
+def sweep_kernel(d_ref, o_ref, p_ref):
+    count, order, _ = d_ref.shape
+    o_ref[...] = d_ref[...]
+    lane = lax.broadcasted_iota(jnp.int32, (PIVOT, PIVOT), 1)
+    sub = lax.broadcasted_iota(jnp.int32, (PIVOT, PIVOT), 0)
+    lane_row = lax.broadcasted_iota(jnp.int32, (1, PIVOT), 1)
+    for blk in range(order // PIVOT):
+        lo = blk * PIVOT
+        p_ref[...] = o_ref[:, lo:lo + PIVOT, lo:lo + PIVOT]
+
+        def step(k, carry):
+            for b in range(count):
+                row = p_ref[b, pl.ds(k, 1), :]
+                piv = jnp.sum(jnp.where(lane_row == k, row, 0.0), axis=1, keepdims=True)
+                inv = 1.0 / piv
+                col = jnp.transpose(jnp.broadcast_to(row, (8, PIVOT)))[:, 0:1]
+                scaled = row * inv
+                mat = p_ref[b]
+                upd = mat - col * scaled
+                upd = jnp.where(lane == k, col * inv, upd)
+                upd = jnp.where(sub == k, jnp.broadcast_to(scaled, (PIVOT, PIVOT)), upd)
+                upd = jnp.where((sub == k) & (lane == k), jnp.broadcast_to(-inv, (PIVOT, PIVOT)), upd)
+                p_ref[b] = upd
+            return carry
+
+        lax.fori_loop(0, PIVOT, step, 0)
+        for b in range(count):
+            pneg = p_ref[b]
+            col_blk = o_ref[b, :, lo:lo + PIVOT]
+            row_blk = o_ref[b, lo:lo + PIVOT, :]
+            t = jnp.dot(col_blk, pneg, precision=PRECISE, preferred_element_type=jnp.float32)
+            o_ref[b] = o_ref[b] + jnp.dot(t, row_blk, precision=PRECISE, preferred_element_type=jnp.float32)
+            o_ref[b, :, lo:lo + PIVOT] = -t
+            o_ref[b, lo:lo + PIVOT, :] = -jnp.dot(pneg, row_blk, precision=PRECISE, preferred_element_type=jnp.float32)
+            o_ref[b, lo:lo + PIVOT, lo:lo + PIVOT] = pneg
+
+
+def negated_inverse(mats):
+    count, order, _ = mats.shape
+    return pl.pallas_call(
+        sweep_kernel,
+        out_shape=jax.ShapeDtypeStruct(mats.shape, mats.dtype),
+        in_specs=[pl.BlockSpec(memory_space=pltpu.VMEM)],
+        out_specs=pl.BlockSpec(memory_space=pltpu.VMEM),
+        scratch_shapes=[pltpu.VMEM((count, PIVOT, PIVOT), jnp.float32)],
+    )(mats)
+
+
+def eliminate(diagonal, coupling, right_side, next_coupling):
+    inverse = -negated_inverse(diagonal)
+    ahead = jnp.einsum("bij,bjk->bik", next_coupling, inverse, precision=PRECISE)
+    behind = jnp.einsum("bji,bjk->bik", coupling, inverse, precision=PRECISE)
     to_next = (
-        jnp.dot(right_part.T, right_part, precision=PRECISE),
-        jnp.dot(right_part.T, left_part, precision=PRECISE),
-        jnp.dot(right_part.T, solved_rhs, precision=PRECISE),
+        jnp.einsum("bik,bjk->bij", ahead, next_coupling, precision=PRECISE),
+        jnp.einsum("bik,bkj->bij", ahead, coupling, precision=PRECISE),
+        jnp.einsum("bik,bk->bi", ahead, right_side, precision=PRECISE),
     )
     to_prev = (
-        jnp.dot(left_part.T, left_part, precision=PRECISE),
-        jnp.dot(left_part.T, solved_rhs, precision=PRECISE),
+        jnp.einsum("bik,bkj->bij", behind, coupling, precision=PRECISE),
+        jnp.einsum("bik,bk->bi", behind, right_side, precision=PRECISE),
     )
     return (to_next, to_prev)
 
@@ -143,13 +189,11 @@
         cam_rhs - schur_vec[:, :blocks] - jnp.pad(spill_vec, ((0, 0), (0, blocks - border)))
     )
     after_coupling = passed_along(coupling[0], "tm", -1)
-    pair = jax.vmap(eliminate)(
-        (
-            jnp.stack([diagonal[1], diagonal[3]]),
-            jnp.stack([coupling[1], coupling[3]]),
-            jnp.stack([right_side[1], right_side[3]]),
-            jnp.stack([coupling[2], after_coupling]),
-        )
+    pair = eliminate(
+        jnp.stack([diagonal[1], diagonal[3]]),
+        jnp.stack([coupling[1], coupling[3]]),
+        jnp.stack([right_side[1], right_side[3]]),
+        jnp.stack([coupling[2], after_coupling]),
     )
     next_first, prev_first = jax.tree.map(lambda x: x[0], pair)
     next_last, prev_last = jax.tree.map(lambda x: x[1], pair)
@@ -157,7 +201,10 @@
     mid_coupling = -next_first[1]
     mid_rhs = right_side[2] - next_first[2] - prev_last[1]
     arrived_last = passed_along((next_last[0], next_last[2]), "tm", 1)
-    next_mid, prev_mid = eliminate((mid_diag, mid_coupling, mid_rhs, -next_last[1]))
+    next_mid, prev_mid = jax.tree.map(
+        lambda x: x[0],
+        eliminate(mid_diag[None], mid_coupling[None], mid_rhs[None], -next_last[1][None]),
+    )
     head_diag = diagonal[0] - prev_first[0] - prev_mid[0] - arrived_last[0]
     head_rhs = right_side[0] - prev_first[1] - prev_mid[1] - arrived_last[1]
     arrived = passed_along((next_mid[0], next_mid[1], next_mid[2]), "tm", 1)

time: 572 us -> 507 us (0.89)
  Pallas kernels: 0 us -> 279 us
  other arithmetic: 295 us -> 16.7 us
  local copies, waits for them, and re-layouts: 60.6 us -> 18.5 us
  matrix products: 66.6 us -> 53.2 us
    pallas_call x0 -> x2, Pallas kernels: none -> 279 us  [negated_inverse(): pl.pallas_call(sweep_kernel, out_shape=jax.ShapeDtypeStruct(mats.shape, m...]
    another operation x31 -> x0, other arithmetic: 275 us -> none  [the longest x25 181 us: eliminate(): factor = jnp.linalg.cholesky(diagonal)]
    another operation x30 -> x0, local copies, waits for them, and re-layouts: 28 us -> none
    another operation x18 -> x0, matrix products: 18.4 us -> none  [the longest x8 11.3 us: eliminate(): factor = jnp.linalg.cholesky(diagonal)]
    unnamed x80 -> x31, local copies, waits for them, and re-layouts: 9.42 us -> 3.13 us
    dot_general x16 -> x14, matrix products: 24 us -> 25 us  [the longest x2 5.12 us: eliminate(): behind = jnp.einsum('bji,bjk->bik', coupling, inverse, precision=PRECISE)]
  transfers between devices with their start and end apart: 9 -> 9, of which waited for: 6 -> 6; matrix products, arithmetic and copies ran while one was open for 8% -> 3% of each run, Pallas kernels for 0% -> 37%
where the time goes in v3:
time: 507 us; the launch traced here: 498 us
  Pallas kernels  279 us (55%)
  waiting for transfers between devices  98.1 us (19%)
  matrix products  53.2 us (10%)
  local copies, waits for them, and re-layouts  18.5 us (4%)
  other arithmetic  16.7 us (3%)
  between operations  14.9 us (3%)
  starting transfers between devices  9.27 us (2%)
  blocking collectives  8.76 us (2%)
    pallas_call x2, Pallas kernels, negated_inverse(): pl.pallas_call(sweep_kernel, out_shape=jax.ShapeDtypeStruct(mats.shape, m...  279 us
    psum x1, waiting for transfers between devices, local(): schur_mat, schur_vec = lax.psum((schur_mat, schur_vec), 'lm')  55.1 us
    ppermute x8, waiting for transfers between devices, passed_along(): return lax.ppermute(block, axis, route)  42.9 us
    dot_general x1, matrix products, one_group(): jnp.einsum('ersl,frsl->sef', placed_cam, placed_proj, precision=PRECISE)  13.3 us
  transfers between devices with their start and end apart: 9, of which 6 were waited for; matrix products, arithmetic and copies ran while one was open for 3% of the time, Pallas kernels for 37%

profile of v3, /device:TPU:0, one launch (start us, length us, event | category | flops | bytes accessed | tf_op | source)
XLA Modules:
  0.0 498.2 jit_solution(14052020083625640140)
XLA Ops:
  9.1 1.7 fusion.7
  11.6 4.3 subtract_reduce_fusion.7
  22.7 3.4 convolution_bitcast_fusion
  26.1 3.1 convolution_bitcast_fusion.1
  29.2 3.6 copy.60
  32.8 2.8 copy.75
  35.6 3.6 copy.74
  39.3 13.3 %fusion.4 = f32[4,402,402]{2,1,0:T(8,128)} fusion(f32[402,4,4,32]{0,3,1,2:T(8,128)} %copy.75, f32[402,4,4,32]{3,2,1,0:T(4,128)S(1)} %bitcast.147), kind=kOutput, calls=%fused_computation.9 | convolution fusion | flops 992894976 | bytes 4232256 | tf_op jit(solution)/shard_map/while/body/eval_jaxpr/ersl,frsl->sef/dot_general | solution.py:80
  57.1 8.8 %psum.15 = f32[4,402]{1,0:T(4,128)S(1)} all-reduce(f32[4,402]{1,0:T(4,128)S(1)} %bitcast.163), channel_id=1, replica_groups=mesh['tm'=8,'lm'=4] {'lm'}, use_global_device_ids=true, to_apply=%region_1.0 | all-reduce | flops 1608 | bytes 12864 | tf_op jit(solution)/shard_map/psum | solution.py:174
  65.9 1.6 collective-permute-start.5
  67.4 4.7 collective-permute-done.5
  72.2 55.1 %all-reduce.5.cloned.1.call-done = f32[4,402,402]{2,1,0:T(8,128)} async-done(((f32[4,402,402]{2,1,0:T(8,128)}), f32[4,402,402]{2,1,0:T(8,128)}) %all-reduce.5.cloned.1.call-update) | async-done | bytes 2585680 | tf_op jit(solution)/shard_map/psum | solution.py:174
  128.1 1.5 collective-permute-start
  130.5 4.4 collective-permute-done
  134.9 3.5 fusion.2
  139.6 1.5 collective-permute-start.1
  142.3 184.9 %shard_map.103 = f32[2,384,384]{2,1,0:T(8,128)} custom-call(f32[2,384,384]{2,1,0:T(8,128)} %pad_maximum_fusion.1.d_ref), custom_call_target="tpu_custom_call" | custom-call | tf_op jit(solution)/shard_map/pallas_call | solution.py:140
  327.2 3.8 fusion.10
  332.8 2.4 fusion.14
  335.2 2.4 fusion.8
  337.6 2.8 fusion.12
  340.4 2.4 fusion.13
  344.0 2.0 slice_bitcast_fusion
  346.0 93.8 %shard_map.104 = f32[1,384,384]{2,1,0:T(8,128)} custom-call(f32[1,384,384]{2,1,0:T(8,128)} %get-tuple-element.42.d_ref), custom_call_target="tpu_custom_call" | custom-call | tf_op jit(solution)/shard_map/pallas_call | solution.py:140
  439.8 2.4 fusion.21
  442.3 1.4 fusion.23
  444.3 1.3 fusion.30
  448.6 1.4 collective-permute-start.4
  450.1 1.5 collective-permute-start.2
  454.4 24.7 %collective-permute-done.4 = f32[384,384]{1,0:T(8,128)S(1)} collective-permute-done((f32[384,384]{1,0:T(8,128)S(1)}, f32[384,384]{1,0:T(8,128)S(1)}, u32[]{:S(2)}, u32[]{:S(2)}) %collective-permute-start.4) | collective-permute-done | bytes 589856 | tf_op jit(solution)/shard_map/ppermute | solution.py:19
  479.9 8.8 %collective-permute-done.2 = f32[384,384]{1,0:T(8,128)S(1)} collective-permute-done((f32[384,384]{1,0:T(8,128)S(1)}, f32[384,384]{1,0:T(8,128)S(1)}, u32[]{:S(2)}, u32[]{:S(2)}) %collective-permute-start.2) | collective-permute-done | bytes 589856 | tf_op jit(solution)/shard_map/ppermute | solution.py:19
  488.8 2.1 fusion.20
  (89 shorter events, 28.2 us)
Async XLA Ops:
  7.2 8.8 %copy-start.11 = (s32[4,32]{1,0:T(4,128)S(1)}, s32[4,32]{1,0:T(4,128)}, u32[]{:S(2)}) copy-start(s32[4,32]{1,0:T(4,128)} %param.15) | copy-start | bytes 1540
  7.2 120.2 %all-reduce.5.cloned.1.call-start = ((), (), s32[]{:S(2)}) async-start(), calls=%async_computation | async-start | bytes 6684672 | tf_op jit(solution)/shard_map/psum | solution.py:174
  9.1 8.6 %copy-start.4 = (f32[4,24,4,32]{3,2,1,0:T(4,128)S(1)}, f32[4,24,4,32]{3,2,1,0:T(4,128)}, u32[]{:S(2)}) copy-start(f32[4,24,4,32]{3,2,1,0:T(4,128)} %param.11) | copy-start | bytes 147460
  17.7 3.3 copy-start.5
  21.3 1.4 copy-start.7
  52.6 0.7 copy-start.8
  52.6 1.8 copy-start.6
  52.6 3.8 copy-start.2
  54.4 17.8 %copy-start.10 = (f32[4,384]{1,0:T(4,128)S(1)}, f32[4,384]{1,0:T(4,128)}, u32[]{:S(2)}) copy-start(f32[4,384]{1,0:T(4,128)} %param.10) | copy-start | bytes 18436
  65.9 6.3 %collective-permute-start.5 = (f32[18]{0:T(128)S(1)}, f32[18]{0:T(128)S(1)}, u32[]{:S(2)}, u32[]{:S(2)}) collective-permute-start(f32[18]{0:T(128)S(1)} %slice_bitcast_fusion.3), channel_id=1, source_target_pairs={{28,0},{0,4},{4,8},{8,12},{12,16},{16,20},{20,24},{24,28},{29,1},{... | collective-permute-start | bytes 224 | tf_op jit(solution)/shard_map/ppermute | solution.py:19
  128.1 6.8 %collective-permute-start = (f32[18,402]{1,0:T(8,128)S(1)}, f32[18,402]{1,0:T(8,128)S(1)}, u32[]{:S(2)}, u32[]{:S(2)}) collective-permute-start(f32[18,402]{1,0:T(8,128)S(1)} %slice_bitcast_fusion.2), channel_id=1, source_target_pairs={{28,0},{0,4},{4,8},{8,12},{12,16},{16,20},{20,24},{24,28},{29,1},{... | collective-permute-start | bytes 86840 | tf_op jit(solution)/shard_map/ppermute | solution.py:19
  138.5 2.7 copy-start.1
  139.6 195.5 %collective-permute-start.1 = (f32[384,384]{1,0:T(8,128)}, f32[384,384]{1,0:T(8,128)S(1)}, u32[]{:S(2)}, u32[]{:S(2)}) collective-permute-start(f32[384,384]{1,0:T(8,128)} %get-tuple-element.36), channel_id=1, source_target_pairs={{4,0},{8,4},{12,8},{16,12},{20,16},{24,20},{28,24},{0,28},{5,1},{9... | collective-permute-start | bytes 1769480 | tf_op jit(solution)/shard_map/ppermute | solution.py:19
  332.8 2.4 copy-start
  439.8 2.4 copy-start.3
  446.9 6.6 %collective-permute-start.6 = (f32[384]{0:T(512)S(1)}, f32[384]{0:T(512)S(1)}, u32[]{:S(2)}, u32[]{:S(2)}) collective-permute-start(f32[384]{0:T(512)S(1)} %slice_reduce_fusion), channel_id=1, source_target_pairs={{28,0},{0,4},{4,8},{8,12},{12,16},{16,20},{20,24},{24,28},{29,1},{... | collective-permute-start | bytes 4616 | tf_op jit(solution)/shard_map/ppermute | solution.py:19
  447.4 6.4 %collective-permute-start.7 = (f32[384]{0:T(512)S(1)}, f32[384]{0:T(512)S(1)}, u32[]{:S(2)}, u32[]{:S(2)}) collective-permute-start(f32[384]{0:T(512)S(1)} %convolution_reduce_fusion), channel_id=1, source_target_pairs={{28,0},{0,4},{4,8},{8,12},{12,16},{16,20},{20,24},{24,28},{29,1},{... | collective-permute-start | bytes 4616 | tf_op jit(solution)/shard_map/ppermute | solution.py:19
  447.5 32.4 %collective-permute-start.3 = (f32[384,384]{1,0:T(8,128)S(1)}, f32[384,384]{1,0:T(8,128)S(1)}, u32[]{:S(2)}, u32[]{:S(2)}) collective-permute-start(f32[384,384]{1,0:T(8,128)S(1)} %fusion.27), channel_id=1, source_target_pairs={{28,0},{0,4},{4,8},{8,12},{12,16},{16,20},{20,24},{24,28},{29,1},{... | collective-permute-start | bytes 1769480 | tf_op jit(solution)/shard_map/ppermute | solution.py:19
  448.6 30.5 %collective-permute-start.4 = (f32[384,384]{1,0:T(8,128)S(1)}, f32[384,384]{1,0:T(8,128)S(1)}, u32[]{:S(2)}, u32[]{:S(2)}) collective-permute-start(f32[384,384]{1,0:T(8,128)S(1)} %fusion.30), channel_id=1, source_target_pairs={{28,0},{0,4},{4,8},{8,12},{12,16},{16,20},{20,24},{24,28},{29,1},{... | collective-permute-start | bytes 1769480 | tf_op jit(solution)/shard_map/ppermute | solution.py:19
  450.1 3.7 copy-start.9
  450.1 38.7 %collective-permute-start.2 = (f32[384,384]{1,0:T(8,128)S(1)}, f32[384,384]{1,0:T(8,128)S(1)}, u32[]{:S(2)}, u32[]{:S(2)}) collective-permute-start(f32[384,384]{1,0:T(8,128)S(1)} %get-tuple-element.41), channel_id=1, source_target_pairs={{28,0},{0,4},{4,8},{8,12},{12,16},{16,20},{20,24},{24,28},{29,1},{... | collective-permute-start | bytes 1769480 | tf_op jit(solution)/shard_map/ppermute | solution.py:19
Sparse Core Ops, SparseCore 0:
  52.7 74.5 all-reduce.4

commit v4 on v3

--- a/solution.py
+++ b/solution.py
@@ -101,8 +101,6 @@
 def sweep_kernel(d_ref, o_ref, p_ref):
     count, order, _ = d_ref.shape
     o_ref[...] = d_ref[...]
-    lane = lax.broadcasted_iota(jnp.int32, (PIVOT, PIVOT), 1)
-    sub = lax.broadcasted_iota(jnp.int32, (PIVOT, PIVOT), 0)
     lane_row = lax.broadcasted_iota(jnp.int32, (1, PIVOT), 1)
     for blk in range(order // PIVOT):
         lo = blk * PIVOT
@@ -111,16 +109,16 @@
         def step(k, carry):
             for b in range(count):
                 row = p_ref[b, pl.ds(k, 1), :]
-                piv = jnp.sum(jnp.where(lane_row == k, row, 0.0), axis=1, keepdims=True)
+                is_k = lane_row == k
+                piv = jnp.sum(jnp.where(is_k, row, 0.0), axis=1, keepdims=True)
                 inv = 1.0 / piv
-                col = jnp.transpose(jnp.broadcast_to(row, (8, PIVOT)))[:, 0:1]
                 scaled = row * inv
-                mat = p_ref[b]
-                upd = mat - col * scaled
-                upd = jnp.where(lane == k, col * inv, upd)
-                upd = jnp.where(sub == k, jnp.broadcast_to(scaled, (PIVOT, PIVOT)), upd)
-                upd = jnp.where((sub == k) & (lane == k), jnp.broadcast_to(-inv, (PIVOT, PIVOT)), upd)
-                p_ref[b] = upd
+                col = jnp.broadcast_to(
+                    jnp.transpose(jnp.broadcast_to(row, (8, PIVOT)))[:, 0:1], (PIVOT, PIVOT)
+                )
+                upd = p_ref[b] - col * scaled
+                p_ref[b] = jnp.where(is_k, col * inv, upd)
+                p_ref[b, pl.ds(k, 1), :] = jnp.where(is_k, -inv, scaled)
             return carry
 
         lax.fori_loop(0, PIVOT, step, 0)

time: 507 us -> 475 us (0.937)
  Pallas kernels: 279 us -> 247 us
    pallas_call x2, Pallas kernels: 279 us -> 247 us  [negated_inverse(): pl.pallas_call(sweep_kernel, out_shape=jax.ShapeDtypeStruct(mats.shape, m...]
  transfers between devices with their start and end apart: 9 -> 9, of which waited for: 6 -> 6; matrix products, arithmetic and copies ran while one was open for 3% -> 4% of each run, Pallas kernels for 37% -> 36%
where the time goes in v4:
time: 475 us; the launch traced here: 466 us
  Pallas kernels  247 us (52%)
  waiting for transfers between devices  98.1 us (21%)
  matrix products  53.2 us (11%)
  local copies, waits for them, and re-layouts  18.5 us (4%)
  other arithmetic  16.7 us (4%)
  between operations  14.9 us (3%)
  starting transfers between devices  9.28 us (2%)
  blocking collectives  8.76 us (2%)
    pallas_call x2, Pallas kernels, negated_inverse(): pl.pallas_call(sweep_kernel, out_shape=jax.ShapeDtypeStruct(mats.shape, m...  247 us
    psum x1, waiting for transfers between devices, local(): schur_mat, schur_vec = lax.psum((schur_mat, schur_vec), 'lm')  55.1 us
    ppermute x8, waiting for transfers between devices, passed_along(): return lax.ppermute(block, axis, route)  42.9 us
    dot_general x1, matrix products, one_group(): jnp.einsum('ersl,frsl->sef', placed_cam, placed_proj, precision=PRECISE)  13.3 us
  transfers between devices with their start and end apart: 9, of which 6 were waited for; matrix products, arithmetic and copies ran while one was open for 4% of the time, Pallas kernels for 36%

profile of v4, /device:TPU:0, one launch (start us, length us, event | category | flops | bytes accessed | tf_op | source)
XLA Modules:
  0.0 466.0 jit_solution(9983108347653043692)
XLA Ops:
  9.1 1.7 fusion.7
  11.6 4.3 subtract_reduce_fusion.7
  22.7 3.4 convolution_bitcast_fusion
  26.1 3.1 convolution_bitcast_fusion.1
  29.2 3.6 copy.60
  32.8 2.8 copy.75
  35.6 3.6 copy.74
  39.3 13.3 %fusion.4 = f32[4,402,402]{2,1,0:T(8,128)} fusion(f32[402,4,4,32]{0,3,1,2:T(8,128)} %copy.75, f32[402,4,4,32]{3,2,1,0:T(4,128)S(1)} %bitcast.147), kind=kOutput, calls=%fused_computation.9 | convolution fusion | flops 992894976 | bytes 4232256 | tf_op jit(solution)/shard_map/while/body/eval_jaxpr/ersl,frsl->sef/dot_general | solution.py:80
  57.1 8.8 %psum.15 = f32[4,402]{1,0:T(4,128)S(1)} all-reduce(f32[4,402]{1,0:T(4,128)S(1)} %bitcast.163), channel_id=1, replica_groups=mesh['tm'=8,'lm'=4] {'lm'}, use_global_device_ids=true, to_apply=%region_1.0 | all-reduce | flops 1608 | bytes 12864 | tf_op jit(solution)/shard_map/psum | solution.py:172
  65.9 1.6 collective-permute-start.5
  67.4 4.7 %collective-permute-done.5 = f32[18]{0:T(128)S(1)} collective-permute-done((f32[18]{0:T(128)S(1)}, f32[18]{0:T(128)S(1)}, u32[]{:S(2)}, u32[]{:S(2)}) %collective-permute-start.5) | collective-permute-done | bytes 104 | tf_op jit(solution)/shard_map/ppermute | solution.py:19
  72.2 55.1 %all-reduce.5.cloned.1.call-done = f32[4,402,402]{2,1,0:T(8,128)} async-done(((f32[4,402,402]{2,1,0:T(8,128)}), f32[4,402,402]{2,1,0:T(8,128)}) %all-reduce.5.cloned.1.call-update) | async-done | bytes 2585680 | tf_op jit(solution)/shard_map/psum | solution.py:172
  128.1 1.5 collective-permute-start
  130.5 4.4 collective-permute-done
  134.9 3.5 fusion.2
  139.6 1.5 collective-permute-start.1
  142.3 168.4 %shard_map.103 = f32[2,384,384]{2,1,0:T(8,128)} custom-call(f32[2,384,384]{2,1,0:T(8,128)} %pad_maximum_fusion.1.d_ref), custom_call_target="tpu_custom_call" | custom-call | tf_op jit(solution)/shard_map/pallas_call | solution.py:138
  310.7 3.8 fusion.10
  316.3 2.4 fusion.14
  318.7 2.4 fusion.8
  321.2 2.8 fusion.12
  324.0 2.4 fusion.13
  327.5 2.0 slice_bitcast_fusion
  329.6 78.1 %shard_map.104 = f32[1,384,384]{2,1,0:T(8,128)} custom-call(f32[1,384,384]{2,1,0:T(8,128)} %get-tuple-element.42.d_ref), custom_call_target="tpu_custom_call" | custom-call | tf_op jit(solution)/shard_map/pallas_call | solution.py:138
  407.6 2.4 fusion.21
  410.1 1.4 fusion.23
  412.1 1.3 fusion.30
  416.4 1.5 collective-permute-start.4
  417.9 1.5 collective-permute-start.2
  422.2 24.7 %collective-permute-done.4 = f32[384,384]{1,0:T(8,128)S(1)} collective-permute-done((f32[384,384]{1,0:T(8,128)S(1)}, f32[384,384]{1,0:T(8,128)S(1)}, u32[]{:S(2)}, u32[]{:S(2)}) %collective-permute-start.4) | collective-permute-done | bytes 589856 | tf_op jit(solution)/shard_map/ppermute | solution.py:19
  447.8 8.8 %collective-permute-done.2 = f32[384,384]{1,0:T(8,128)S(1)} collective-permute-done((f32[384,384]{1,0:T(8,128)S(1)}, f32[384,384]{1,0:T(8,128)S(1)}, u32[]{:S(2)}, u32[]{:S(2)}) %collective-permute-start.2) | collective-permute-done | bytes 589856 | tf_op jit(solution)/shard_map/ppermute | solution.py:19
  456.6 2.1 fusion.20
  (89 shorter events, 28.2 us)
Async XLA Ops:
  7.2 8.8 %copy-start.11 = (s32[4,32]{1,0:T(4,128)S(1)}, s32[4,32]{1,0:T(4,128)}, u32[]{:S(2)}) copy-start(s32[4,32]{1,0:T(4,128)} %param.15) | copy-start | bytes 1540
  7.2 120.2 %all-reduce.5.cloned.1.call-start = ((), (), s32[]{:S(2)}) async-start(), calls=%async_computation | async-start | bytes 6684672 | tf_op jit(solution)/shard_map/psum | solution.py:172
  9.1 8.6 %copy-start.4 = (f32[4,24,4,32]{3,2,1,0:T(4,128)S(1)}, f32[4,24,4,32]{3,2,1,0:T(4,128)}, u32[]{:S(2)}) copy-start(f32[4,24,4,32]{3,2,1,0:T(4,128)} %param.11) | copy-start | bytes 147460
  17.7 3.3 copy-start.5
  21.3 1.4 copy-start.7
  52.6 0.7 copy-start.8
  52.6 1.8 copy-start.6
  52.6 3.8 copy-start.2
  54.4 17.8 %copy-start.10 = (f32[4,384]{1,0:T(4,128)S(1)}, f32[4,384]{1,0:T(4,128)}, u32[]{:S(2)}) copy-start(f32[4,384]{1,0:T(4,128)} %param.10) | copy-start | bytes 18436
  65.9 6.3 %collective-permute-start.5 = (f32[18]{0:T(128)S(1)}, f32[18]{0:T(128)S(1)}, u32[]{:S(2)}, u32[]{:S(2)}) collective-permute-start(f32[18]{0:T(128)S(1)} %slice_bitcast_fusion.3), channel_id=1, source_target_pairs={{28,0},{0,4},{4,8},{8,12},{12,16},{16,20},{20,24},{24,28},{29,1},{... | collective-permute-start | bytes 224 | tf_op jit(solution)/shard_map/ppermute | solution.py:19
  128.1 6.8 %collective-permute-start = (f32[18,402]{1,0:T(8,128)S(1)}, f32[18,402]{1,0:T(8,128)S(1)}, u32[]{:S(2)}, u32[]{:S(2)}) collective-permute-start(f32[18,402]{1,0:T(8,128)S(1)} %slice_bitcast_fusion.2), channel_id=1, source_target_pairs={{28,0},{0,4},{4,8},{8,12},{12,16},{16,20},{20,24},{24,28},{29,1},{... | collective-permute-start | bytes 86840 | tf_op jit(solution)/shard_map/ppermute | solution.py:19
  138.5 2.7 copy-start.1
  139.6 179.1 %collective-permute-start.1 = (f32[384,384]{1,0:T(8,128)}, f32[384,384]{1,0:T(8,128)S(1)}, u32[]{:S(2)}, u32[]{:S(2)}) collective-permute-start(f32[384,384]{1,0:T(8,128)} %get-tuple-element.36), channel_id=1, source_target_pairs={{4,0},{8,4},{12,8},{16,12},{20,16},{24,20},{28,24},{0,28},{5,1},{9... | collective-permute-start | bytes 1769480 | tf_op jit(solution)/shard_map/ppermute | solution.py:19
  316.3 2.4 copy-start
  407.6 2.4 copy-start.3
  414.7 6.6 %collective-permute-start.6 = (f32[384]{0:T(512)S(1)}, f32[384]{0:T(512)S(1)}, u32[]{:S(2)}, u32[]{:S(2)}) collective-permute-start(f32[384]{0:T(512)S(1)} %slice_reduce_fusion), channel_id=1, source_target_pairs={{28,0},{0,4},{4,8},{8,12},{12,16},{16,20},{20,24},{24,28},{29,1},{... | collective-permute-start | bytes 4616 | tf_op jit(solution)/shard_map/ppermute | solution.py:19
  415.3 6.4 %collective-permute-start.7 = (f32[384]{0:T(512)S(1)}, f32[384]{0:T(512)S(1)}, u32[]{:S(2)}, u32[]{:S(2)}) collective-permute-start(f32[384]{0:T(512)S(1)} %convolution_reduce_fusion), channel_id=1, source_target_pairs={{28,0},{0,4},{4,8},{8,12},{12,16},{16,20},{20,24},{24,28},{29,1},{... | collective-permute-start | bytes 4616 | tf_op jit(solution)/shard_map/ppermute | solution.py:19
  415.3 32.4 %collective-permute-start.3 = (f32[384,384]{1,0:T(8,128)S(1)}, f32[384,384]{1,0:T(8,128)S(1)}, u32[]{:S(2)}, u32[]{:S(2)}) collective-permute-start(f32[384,384]{1,0:T(8,128)S(1)} %fusion.27), channel_id=1, source_target_pairs={{28,0},{0,4},{4,8},{8,12},{12,16},{16,20},{20,24},{24,28},{29,1},{... | collective-permute-start | bytes 1769480 | tf_op jit(solution)/shard_map/ppermute | solution.py:19
  416.4 30.5 %collective-permute-start.4 = (f32[384,384]{1,0:T(8,128)S(1)}, f32[384,384]{1,0:T(8,128)S(1)}, u32[]{:S(2)}, u32[]{:S(2)}) collective-permute-start(f32[384,384]{1,0:T(8,128)S(1)} %fusion.30), channel_id=1, source_target_pairs={{28,0},{0,4},{4,8},{8,12},{12,16},{16,20},{20,24},{24,28},{29,1},{... | collective-permute-start | bytes 1769480 | tf_op jit(solution)/shard_map/ppermute | solution.py:19
  417.9 3.8 copy-start.9
  417.9 38.7 %collective-permute-start.2 = (f32[384,384]{1,0:T(8,128)S(1)}, f32[384,384]{1,0:T(8,128)S(1)}, u32[]{:S(2)}, u32[]{:S(2)}) collective-permute-start(f32[384,384]{1,0:T(8,128)S(1)} %get-tuple-element.41), channel_id=1, source_target_pairs={{28,0},{0,4},{4,8},{8,12},{12,16},{16,20},{20,24},{24,28},{29,1},{... | collective-permute-start | bytes 1769480 | tf_op jit(solution)/shard_map/ppermute | solution.py:19
Sparse Core Ops, SparseCore 0:
  52.7 74.5 all-reduce.4
